TPU v7x, 256 devices: a whole 4x4x8 slice. The times are simulated.
256 devices in a mesh: rep: 16 (over z_lo, x), shard: 16 (over z_hi, y, core).
Axes of the slice: x: 4, y: 4, z: 8 (z_hi: 2, z_lo: 4; z = z_hi * 4 + z_lo), core: 2. Of those that a mesh axis runs over, the one named last changes fastest.
Arguments:
- attn: bfloat16 [16, 6144, 2560], P('rep', 'shard'), may hold values from -6 to 6
- resid: bfloat16 [16, 6144, 2560], P('rep', 'shard'), may hold values from -200 to 200
- cotangent: bfloat16 [16, 6144, 2560], P('rep', 'shard'), may hold values from -6 to 6
- gain: float32 [2560], replicated, may hold values from 0.1 to 1.9
- numer: float32 [16, 2560, 2560], P('rep', 'shard'), may hold values from -6 to 6
- pweight: float32 [16], P('rep'), may hold values from 0.5 to 2
- round_bit: int32 [1], replicated, may hold values from 0 to 3
Outputs:
- new_numer: float32 [16, 2560, 2560], P('rep', 'shard')
- new_pweight: float32 [16], P('rep')
All inputs are finite; a program needn't handle non-finite values.
Results may differ from a plain program's by a relative error of at most 0.008.
Values may be sent and summed in bfloat16 or wider, within the bound.
No kernel may reach another device: no remote copies, remote signals or barrier semaphores. Data moves between devices by JAX's collectives and lax.ppermute only.
A program may use at most 192 MiB of HBM per device.

v0:
```python
import jax
import jax.numpy as jnp
from jax import lax
from jax.sharding import PartitionSpec as P

EPS = 1e-05
learning_rate = 0.5


def shortened(shard):

    def short(part):
        return part.astype(jnp.bfloat16) if part.dtype == jnp.float32 else part

    return jax.tree.map(short, shard)


def from_partner(shard, axis, apart):
    return lax.ppermute(shard, axis, [(i, i ^ 1 << apart) for i in range(lax.axis_size(axis))])


def on_device(attn, resid, cotangent, gain, numer, pweight, round_bit):
    acts = attn[0]
    weight_rows = (numer[0] / pweight[0]).astype(jnp.bfloat16)
    columns = acts
    pre = resid[0].astype(jnp.float32) + jnp.dot(
        columns,
        lax.all_gather(weight_rows, "shard", axis=0, tiled=True),
        preferred_element_type=jnp.float32,
    )
    inv = lax.rsqrt(jnp.mean(pre * pre, axis=1, keepdims=True) + EPS)
    normed = pre * inv
    dnorm = cotangent[0].astype(jnp.float32) * gain
    dpre = (inv * (dnorm - normed * jnp.mean(dnorm * normed, axis=1, keepdims=True))).astype(
        jnp.bfloat16
    )
    columns = acts
    grad = lax.psum_scatter(
        lax.dot_general(
            columns, dpre, (((0,), (0,)), ((), ())), preferred_element_type=jnp.float32
        ).astype(jnp.bfloat16),
        "shard",
        scatter_dimension=0,
        tiled=True,
    ).astype(jnp.float32)
    stepped = numer[0] - learning_rate * grad
    levels = lax.axis_size("rep").bit_length() - 1

    def pushed(bit):

        def send_pair(pair):
            return jax.tree.map(
                lambda part, own: part.astype(own.dtype),
                from_partner(shortened(pair), "rep", bit),
                pair,
            )

        return send_pair

    other_numer, other_weight = lax.switch(
        round_bit[0], [pushed(level) for level in range(levels)], (stepped, pweight)
    )
    new_numer = (0.5 * (stepped + other_numer))[None]
    new_pweight = 0.5 * (pweight + other_weight)
    return (new_numer, new_pweight)


def solution(mesh):
    in_specs = (
        P("rep", "shard", None),
        P("rep", "shard", None),
        P("rep", "shard", None),
        P(),
        P("rep", "shard", None),
        P("rep"),
        P(),
    )
    out_specs = (P("rep", "shard", None), P("rep"))
    return jax.shard_map(
        on_device, mesh=mesh, in_specs=in_specs, out_specs=out_specs, check_vma=False
    )
```

profile of v0, /device:TPU:2, one launch (start us, length us, event | category | flops | bytes accessed | tf_op | source)
XLA Modules:
  0.0 407.9 jit_solution(1422949947530526747)
XLA Ops:
  7.2 0.0 copy-start
  7.2 0.0 all-gather.2.cloned.1.call-start
  8.0 2.4 fusion.14
  10.4 0.0 all-gather.2.cloned.1.call-update
  10.5 0.0 reduce-scatter.4.cloned.1.call-start
  10.5 4.0 copy.18
  14.5 4.0 copy.19
  18.5 140.7 %all-gather.2.cloned.1.call-done = bf16[2560,2560]{1,0:T(8,128)(2,1)} async-done(((bf16[160,2560]{1,0:T(8,128)(2,1)}), bf16[2560,2560]{1,0:T(8,128)(2,1)}) %all-gather.2.cloned.1.call-update) | async-done | bytes 13107216 | tf_op jit(solution)/shard_map/all_gather | solution.py:28
  159.2 10.8 %multiply_reduce_fusion = (f32[384]{0:T(512)S(1)}, f32[384,2560]{0,1:T(8,128)S(1)}) fusion(bf16[2560,2560]{1,0:T(8,128)(2,1)} %all-gather.2.cloned.1.call-done, bf16[1,384,2560]{2,1,0:T(8,128)(2,1)S(1)} %copy-done, bf16[1,384,2560]{1,2,0:T(8,128)(2,1)} %copy.18), kind=kOutput, calls=%fused_computation.10 | convolution fusion | flops 5037096448 | bytes 20973056 | tf_op jit(solution)/shard_map/dot_general | solution.py:26
  170.0 0.0 copy-done.4
  170.0 0.7 fusion.4
  170.7 10.4 %fusion = bf16[2560,2560]{0,1:T(8,128)(2,1)} fusion(f32[384,2560]{0,1:T(8,128)S(1)} %get-tuple-element.59, bf16[1,384,2560]{1,2,0:T(8,128)(2,1)S(1)} %copy-done.2, bf16[1,384,2560]{2,1,0:T(8,128)(2,1)S(1)} %copy-done, f32[384]{0:T(512)S(1)} %broadcast_multiply_fusion, f32[2560]{0:T(1024)S(1)} %copy-done.4, f32[384]{0:T(512)S(1)} %add_rsqrt_fusion), kind=kOutput, calls=%fused_computation.1 | convolution fusion | flops 5046599680 | bytes 20984832 | tf_op jit(solution)/shard_map/dot_general | solution.py:39
  181.1 17.6 %copy.21 = bf16[2560,2560]{1,0:T(8,128)(2,1)} copy(bf16[2560,2560]{0,1:T(8,128)(2,1)} %fusion) | data formatting | bytes 26214400
  198.8 0.0 reduce-scatter.4.cloned.1.call-update
  199.6 174.4 %reduce-scatter.4.cloned.1.call-done = bf16[160,2560]{1,0:T(8,128)(2,1)} async-done(((bf16[2560,2560]{1,0:T(8,128)(2,1)}), bf16[160,2560]{1,0:T(8,128)(2,1)}) %reduce-scatter.4.cloned.1.call-update) | async-done | bytes 819216 | tf_op jit(solution)/shard_map/reduce_scatter | solution.py:38
  374.0 2.5 bitcast_subtract_fusion
  376.5 20.0 %conditional.4 = (f32[160,2560]{1,0:T(8,128)}, f32[1]{0:T(128)}) conditional(s32[]{:T(128)} %bitcast.7, (f32[160,2560]{1,0:T(8,128)}, f32[1]{0:T(128)}) %tuple.50, (f32[160,2560]{1,0:T(8,128)}, f32[1]{0:T(128)}) %tuple.50, (f32[160,2560]{1,0:T(8,128)}, f32[1]{0:T(128)}) %tuple.50, (f32[160,2560]{1,0:T(8,128)}, ...), branch_computations={%region_3.0_spmd, %region_4.0_spmd, %region_5.0_spmd, %region_6.0_... | conditional | flops 819202 | bytes 8192116
  376.5 1.5 convert_element_type.70
  378.0 0.9 collective-permute-start
  379.6 14.2 %collective-permute-start.1 = (bf16[1]{0:T(256)(128)(2,1)}, bf16[1]{0:T(256)(128)(2,1)}, u32[]{:S(2)}, u32[]{:S(2)}) collective-permute-start(bf16[1]{0:T(256)(128)(2,1)} %convert_element_type.72), channel_id=1, source_target_pairs={{0,16},{16,0},{32,48},{48,32},{64,80},{80,64},{96,112},{112,96},{1... | collective-permute-start | bytes 14 | tf_op jit(solution)/shard_map/cond/branch_0_fun/ppermute | solution.py:19
  393.8 0.8 collective-permute-done.1
  395.1 0.0 collective-permute-done
  395.1 1.4 convert_element_type.108
  396.5 3.4 multiply_bitcast_fusion
  (10 shorter events, 0.0 us)
Async XLA Ops:
  7.2 152.0 %copy-start = (bf16[1,384,2560]{2,1,0:T(8,128)(2,1)S(1)}, bf16[1,384,2560]{2,1,0:T(8,128)(2,1)}, u32[]{:S(2)}) copy-start(bf16[1,384,2560]{2,1,0:T(8,128)(2,1)} %param.11) | copy-start | bytes 5898244
  7.2 152.0 %all-gather.2.cloned.1.call-start = ((), (), s32[]{:S(2)}) async-start(), calls=%async_computation.1 | async-start | bytes 13926400 | tf_op jit(solution)/shard_map/all_gather | solution.py:28
  10.5 363.5 %reduce-scatter.4.cloned.1.call-start = ((), (), s32[]{:S(2)}) async-start(), calls=%async_computation.2 | async-start | bytes 13926400 | tf_op jit(solution)/shard_map/reduce_scatter | solution.py:38
  18.5 151.5 %copy-start.4 = (f32[2560]{0:T(1024)S(1)}, f32[2560]{0:T(1024)}, u32[]{:S(2)}) copy-start(f32[2560]{0:T(1024)} %param.14) | copy-start | bytes 30724
  159.2 10.8 %copy-start.2 = (bf16[1,384,2560]{1,2,0:T(8,128)(2,1)S(1)}, bf16[1,384,2560]{1,2,0:T(8,128)(2,1)}, u32[]{:S(2)}) copy-start(bf16[1,384,2560]{1,2,0:T(8,128)(2,1)} %copy.19) | copy-start | bytes 5898244
  198.8 175.2 %copy-start.3 = (f32[1,160,2560]{2,1,0:T(8,128)S(1)}, f32[1,160,2560]{2,1,0:T(8,128)}, u32[]{:S(2)}) copy-start(f32[1,160,2560]{2,1,0:T(8,128)} %param.15) | copy-start | bytes 4915204
  378.0 17.1 %collective-permute-start = (bf16[160,2560]{1,0:T(8,128)(2,1)S(1)}, bf16[160,2560]{1,0:T(8,128)(2,1)S(1)}, u32[]{:S(2)}, u32[]{:S(2)}) collective-permute-start(bf16[160,2560]{1,0:T(8,128)(2,1)S(1)} %convert_element_type.70), channel_id=1, source_target_pairs={{0,16},{16,0},{32,48},{48,32},{64,80},{80,64},{96,112},{112,96},{1... | collective-permute-start | bytes 2457608 | tf_op jit(solution)/shard_map/cond/branch_0_fun/ppermute | solution.py:19
  379.6 15.0 %collective-permute-start.1 = (bf16[1]{0:T(256)(128)(2,1)}, bf16[1]{0:T(256)(128)(2,1)}, u32[]{:S(2)}, u32[]{:S(2)}) collective-permute-start(bf16[1]{0:T(256)(128)(2,1)} %convert_element_type.72), channel_id=1, source_target_pairs={{0,16},{16,0},{32,48},{48,32},{64,80},{80,64},{96,112},{112,96},{1... | collective-permute-start | bytes 14 | tf_op jit(solution)/shard_map/cond/branch_0_fun/ppermute | solution.py:19
  396.5 3.4 copy-start.1
Sparse Core Ops, SparseCore 0:
  11.3 147.8 all-gather.1
  198.9 174.9 reduce-scatter.3
where the time goes:
time: 411 us; the launch traced here: 408 us
  waiting for transfers between devices  316 us (77%)
  local copies, waits for them, and re-layouts  25.7 us (6%)
  matrix products  21.2 us (5%)
  between operations  16.8 us (4%)
  starting transfers between devices  15.2 us (4%)
  other arithmetic  11.9 us (3%)
    reduce_scatter x1, waiting for transfers between devices, on_device(): lax.psum_scatter(lax.dot_general(columns, dpre, (((0,), (0,)), ((), ())),...  174 us
    all_gather x1, waiting for transfers between devices, on_device(): lax.all_gather(weight_rows, 'shard', axis=0, tiled=True)  141 us
    unnamed x13, local copies, waits for them, and re-layouts  25.7 us
    ppermute x2, starting transfers between devices, from_partner(): lax.ppermute(shard, axis, [(i, i ^ 1 << apart) for i in range(lax.axis_si...  15.1 us
    dot_general x1, matrix products, on_device(): jnp.dot(columns, lax.all_gather(weight_rows, 'shard', axis=0, tiled=True)...  10.8 us
    dot_general x1, matrix products, on_device(): lax.dot_general(columns, dpre, (((0,), (0,)), ((), ())), preferred_elemen...  10.4 us
  transfers between devices with their start and end apart: 4, of which 3 were waited for; matrix products, arithmetic and copies ran while one was open for 2% of the time, Pallas kernels for 0%

commit v1 on v0

v1 whole, which is shorter than its diff:
```python
import jax
import jax.numpy as jnp
import numpy as np
from jax import lax
from jax.sharding import Mesh, PartitionSpec as P

EPS = 1e-05
learning_rate = 0.5


def shortened(shard):

    def short(part):
        return part.astype(jnp.bfloat16) if part.dtype == jnp.float32 else part

    return jax.tree.map(short, shard)


def from_partner(shard, axis, apart):
    return lax.ppermute(shard, axis, [(i, i ^ 1 << apart) for i in range(lax.axis_size(axis))])


def on_device(attn, resid, cotangent, gain, numer, pweight, round_bit):
    n_sh = lax.axis_size("sh")
    n_core = lax.axis_size("core")
    acts = attn[0]
    tok, din = acts.shape
    rows = din // (n_sh * n_core)
    weight_rows = (numer[0] / pweight[0]).astype(jnp.bfloat16)
    me = lax.axis_index("core")
    other = [(i, i ^ 1) for i in range(n_core)]
    w_own = lax.all_gather(weight_rows, "sh", axis=0, tiled=False)
    w_other = lax.ppermute(w_own, "core", other)
    acts4 = acts.reshape(tok, n_sh, n_core, rows)
    a_own = lax.dynamic_index_in_dim(acts4, me, axis=2, keepdims=False)
    a_other = lax.dynamic_index_in_dim(acts4, 1 - me, axis=2, keepdims=False)
    pre = (
        resid[0].astype(jnp.float32)
        + jnp.einsum("tsi,sio->to", a_own, w_own, preferred_element_type=jnp.float32)
        + jnp.einsum("tsi,sio->to", a_other, w_other, preferred_element_type=jnp.float32)
    )
    inv = lax.rsqrt(jnp.mean(pre * pre, axis=1, keepdims=True) + EPS)
    normed = pre * inv
    dnorm = cotangent[0].astype(jnp.float32) * gain
    dpre = (inv * (dnorm - normed * jnp.mean(dnorm * normed, axis=1, keepdims=True))).astype(
        jnp.bfloat16
    )
    part_other = jnp.einsum(
        "tsi,to->sio", a_other, dpre, preferred_element_type=jnp.float32
    ).astype(jnp.bfloat16)
    part_own = jnp.einsum(
        "tsi,to->sio", a_own, dpre, preferred_element_type=jnp.float32
    ).astype(jnp.bfloat16)
    part = part_own + lax.ppermute(part_other, "core", other)
    grad = lax.psum_scatter(part, "sh", scatter_dimension=0, tiled=False).astype(jnp.float32)
    stepped = numer[0] - learning_rate * grad
    levels = lax.axis_size("rep").bit_length() - 1

    def pushed(bit):

        def send_pair(pair):
            return jax.tree.map(
                lambda part, own: part.astype(own.dtype),
                from_partner(shortened(pair), "rep", bit),
                pair,
            )

        return send_pair

    other_numer, other_weight = lax.switch(
        round_bit[0], [pushed(level) for level in range(levels)], (stepped, pweight)
    )
    new_numer = (0.5 * (stepped + other_numer))[None]
    new_pweight = 0.5 * (pweight + other_weight)
    return (new_numer, new_pweight)


def solution(mesh):
    n_rep, n_shard = mesh.devices.shape
    devices = np.asarray(mesh.devices).reshape(n_rep, n_shard // 2, 2)
    split = Mesh(devices, ("rep", "sh", "core"))
    rows = P("rep", ("sh", "core"), None)
    in_specs = (rows, rows, rows, P(), rows, P("rep"), P())
    out_specs = (rows, P("rep"))
    return jax.shard_map(
        on_device, mesh=split, in_specs=in_specs, out_specs=out_specs, check_vma=False
    )
```

time: 411 us -> 381 us (0.927)
  local copies, waits for them, and re-layouts: 25.7 us -> 2.85 us
  other arithmetic: 11.9 us -> 7.16 us
    unnamed x13 -> x7, local copies, waits for them, and re-layouts: 25.7 us -> 2.85 us
    reduce_scatter x1, waiting for transfers between devices: 174 us -> 154 us  [on_device(): lax.psum_scatter(part, 'sh', scatter_dimension=0, tiled=False)]
    ppermute x0 -> x2, waiting for transfers between devices: none -> 12.1 us  [the longest x1 10.4 us: on_device(): part = part_own + lax.ppermute(part_other, 'core', other)]
    all_gather x1, waiting for transfers between devices: 141 us -> 147 us  [on_device(): w_own = lax.all_gather(weight_rows, 'sh', axis=0, tiled=False)]
    dot_general x2 -> x4, matrix products: 21.2 us -> 20.7 us  [the longest x1 6.31 us: on_device(): jnp.einsum('tsi,sio->to', a_own, w_own, preferred_element_type=jnp.float32)]
  transfers between devices with their start and end apart: 4 -> 6, of which waited for: 3 -> 5; matrix products, arithmetic and copies ran while one was open for 2% -> 2% of each run, Pallas kernels for 0% -> 0%
where the time goes in v1:
time: 381 us; the launch traced here: 378 us
  waiting for transfers between devices  314 us (82%)
  matrix products  20.7 us (5%)
  between operations  16.7 us (4%)
  starting transfers between devices  15.4 us (4%)
  other arithmetic  7.16 us (2%)
    reduce_scatter x1, waiting for transfers between devices, on_device(): lax.psum_scatter(part, 'sh', scatter_dimension=0, tiled=False)  154 us
    all_gather x1, waiting for transfers between devices, on_device(): w_own = lax.all_gather(weight_rows, 'sh', axis=0, tiled=False)  147 us
    ppermute x2, starting transfers between devices, from_partner(): lax.ppermute(shard, axis, [(i, i ^ 1 << apart) for i in range(lax.axis_si...  15.1 us
    ppermute x1, waiting for transfers between devices, on_device(): part = part_own + lax.ppermute(part_other, 'core', other)  10.4 us
  transfers between devices with their start and end apart: 6, of which 5 were waited for; matrix products, arithmetic and copies ran while one was open for 2% of the time, Pallas kernels for 0%

profile of v1, /device:TPU:2, one launch (start us, length us, event | category | flops | bytes accessed | tf_op | source)
XLA Modules:
  0.0 378.2 jit_solution(4362569037742040738)
XLA Ops:
  7.2 0.0 all-gather.2.cloned.1.call-start
  7.9 2.4 divide_convert_fusion
  10.3 0.0 all-gather.2.cloned.1.call-update
  10.3 0.0 reduce-scatter.2.cloned.1.call-start
  10.3 147.4 %all-gather.2.cloned.1.call-done = bf16[8,160,2560]{2,1,0:T(8,128)(2,1)} async-done(((bf16[1,160,2560]{2,1,0:T(8,128)(2,1)}), bf16[8,160,2560]{2,1,0:T(8,128)(2,1)}) %all-gather.2.cloned.1.call-update) | async-done | bytes 6553616 | tf_op jit(solution)/shard_map/all_gather | solution.py:32
  157.8 2.8 copy.12
  160.6 6.3 %fusion = f32[384,2560]{1,0:T(8,128)S(1)} fusion(bf16[8,160,2560]{2,1,0:T(8,128)(2,1)} %all-gather.2.cloned.1.call-done, bf16[1,384,2560]{2,1,0:T(8,128)(2,1)} %param.12, bf16[384,8,2,160]{0,3,2,1:T(8,128)(2,1)S(1)} %bitcast.41, s32[]{:T(128)S(6)} %select_n.7), kind=kOutput, calls=%fused_computation.4 | convolution fusion | flops 2518548480 | bytes 13434884 | tf_op jit(solution)/shard_map/tsi,sio->to/dot_general | solution.py:39
  166.9 1.7 collective-permute-done.8
  168.6 5.2 %multiply_reduce_fusion = (f32[384]{0:T(512)S(1)}, f32[384,2560]{1,0:T(8,128)S(1)}) fusion(f32[384,2560]{1,0:T(8,128)S(1)} %fusion, bf16[8,160,2560]{2,1,0:T(8,128)(2,1)} %collective-permute-done.8, bf16[384,8,2,160]{0,3,2,1:T(8,128)(2,1)S(1)} %bitcast.42, s32[]{:T(128)S(6)} %select_n.8), kind=kOutput, calls=%fused_computation.12 | convolution fusion | flops 2519531008 | bytes 15402500 | tf_op jit(solution)/shard_map/tsi,sio->to/dot_general | solution.py:40
  173.8 0.8 fusion.4
  174.6 1.0 fusion.7
  175.7 3.8 convolution_convert_fusion
  179.4 0.2 collective-permute-start.9
  179.6 10.4 %collective-permute-done.9 = bf16[8,160,2560]{2,1,0:T(8,128)(2,1)S(1)} collective-permute-done((bf16[8,160,2560]{2,1,0:T(8,128)(2,1)S(1)}, bf16[8,160,2560]{2,1,0:T(8,128)(2,1)S(1)}, u32[]{:S(2)}, u32[]{:S(2)}) %collective-permute-start.9) | collective-permute-done | bytes 6553632 | tf_op jit(solution)/shard_map/ppermute | solution.py:54
  190.1 5.5 %convert_add_fusion = bf16[8,160,2560]{2,1,0:T(8,128)(2,1)} fusion(bf16[8,160,2560]{2,1,0:T(8,128)(2,1)S(1)} %collective-permute-done.9, bf16[384,2560,1]{1,0,2:T(8,128)(2,1)S(1)} %fusion.7, bf16[384,8,2,160]{0,3,2,1:T(8,128)(2,1)S(1)} %bitcast.44, s32[]{:T(128)S(6)} %select_n.7), kind=kOutput, calls=%fused_computation | convolution fusion | flops 2523136000 | bytes 16056324 | tf_op jit(solution)/shard_map/tsi,to->sio/dot_general | solution.py:51
  196.3 153.5 %reduce-scatter.2.cloned.1.call-done = bf16[1,160,2560]{2,1,0:T(8,128)(2,1)} async-done(((bf16[8,160,2560]{2,1,0:T(8,128)(2,1)}), bf16[1,160,2560]{2,1,0:T(8,128)(2,1)}) %reduce-scatter.2.cloned.1.call-update) | async-done | bytes 819216 | tf_op jit(solution)/shard_map/reduce_scatter | solution.py:55
  349.8 1.3 subtract_bitcast_fusion
  351.2 17.6 %conditional.4 = (f32[160,2560]{1,0:T(8,128)S(1)}, f32[1]{0:T(128)}) conditional(s32[]{:T(128)} %bitcast.10, (f32[160,2560]{1,0:T(8,128)S(1)}, f32[1]{0:T(128)}) %tuple.50, (f32[160,2560]{1,0:T(8,128)S(1)}, f32[1]{0:T(128)}) %tuple.50, (f32[160,2560]{1,0:T(8,128)S(1)}, f32[1]{0:T(128)}) %tuple.50, ...), branch_computations={%region_3.4_spmd, %region_4.5_spmd, %region_5.6_spmd, %region_6.7_... | conditional | flops 819202 | bytes 8192116
  351.2 0.1 convert_element_type.72
  351.3 1.0 collective-permute-start
  352.9 14.1 %collective-permute-start.1 = (bf16[1]{0:T(256)(128)(2,1)}, bf16[1]{0:T(256)(128)(2,1)}, u32[]{:S(2)}, u32[]{:S(2)}) collective-permute-start(bf16[1]{0:T(256)(128)(2,1)} %convert_element_type.74), channel_id=1, source_target_pairs={{0,16},{16,0},{32,48},{48,32},{64,80},{80,64},{96,112},{112,96},{1... | collective-permute-start | bytes 14 | tf_op jit(solution)/shard_map/cond/branch_0_fun/ppermute | solution.py:20
  367.1 0.8 collective-permute-done.1
  368.5 0.2 convert_element_type.110
  368.8 1.3 multiply_bitcast_fusion
  (11 shorter events, 0.0 us)
Async XLA Ops:
  7.2 150.6 %all-gather.2.cloned.1.call-start = ((), (), s32[]{:S(2)}) async-start(), calls=%async_computation.1 | async-start | bytes 7372800 | tf_op jit(solution)/shard_map/all_gather | solution.py:32
  10.3 339.5 %reduce-scatter.2.cloned.1.call-start = ((), (), s32[]{:S(2)}) async-start(), calls=%async_computation.2 | async-start | bytes 7372800 | tf_op jit(solution)/shard_map/reduce_scatter | solution.py:55
  157.8 10.9 %collective-permute-start.8 = (bf16[8,160,2560]{2,1,0:T(8,128)(2,1)}, bf16[8,160,2560]{2,1,0:T(8,128)(2,1)}, u32[]{:S(2)}, u32[]{:S(2)}) collective-permute-start(bf16[8,160,2560]{2,1,0:T(8,128)(2,1)} %all-gather.2.cloned.1.call-done), channel_id=1, source_target_pairs={{0,1},{1,0},{2,3},{3,2},{4,5},{5,4},{6,7},{7,6},{8,9},{9,8},{10,11... | collective-permute-start | bytes 19660808 | tf_op jit(solution)/shard_map/ppermute | solution.py:33
  166.9 6.9 %copy-start = (bf16[1,384,2560]{2,1,0:T(8,128)(2,1)S(1)}, bf16[1,384,2560]{2,1,0:T(8,128)(2,1)}, u32[]{:S(2)}) copy-start(bf16[1,384,2560]{2,1,0:T(8,128)(2,1)} %param.13) | copy-start | bytes 5898244
  166.9 6.9 %copy-start.2 = (f32[2560]{0:T(1024)S(1)}, f32[2560]{0:T(1024)}, u32[]{:S(2)}) copy-start(f32[2560]{0:T(1024)} %param.14) | copy-start | bytes 30724
  179.4 10.6 %collective-permute-start.9 = (bf16[8,160,2560]{2,1,0:T(8,128)(2,1)S(1)}, bf16[8,160,2560]{2,1,0:T(8,128)(2,1)S(1)}, u32[]{:S(2)}, u32[]{:S(2)}) collective-permute-start(bf16[8,160,2560]{2,1,0:T(8,128)(2,1)S(1)} %convolution_convert_fusion), channel_id=1, source_target_pairs={{0,1},{1,0},{2,3},{3,2},{4,5},{5,4},{6,7},{7,6},{8,9},{9,8},{10,11... | collective-permute-start | bytes 19660808 | tf_op jit(solution)/shard_map/ppermute | solution.py:54
  195.5 154.3 %copy-start.1 = (f32[1,160,2560]{2,1,0:T(8,128)S(1)}, f32[1,160,2560]{2,1,0:T(8,128)}, u32[]{:S(2)}) copy-start(f32[1,160,2560]{2,1,0:T(8,128)} %param.15) | copy-start | bytes 4915204
  351.3 17.1 %collective-permute-start = (bf16[160,2560]{1,0:T(8,128)(2,1)S(1)}, bf16[160,2560]{1,0:T(8,128)(2,1)S(1)}, u32[]{:S(2)}, u32[]{:S(2)}) collective-permute-start(bf16[160,2560]{1,0:T(8,128)(2,1)S(1)} %convert_element_type.72), channel_id=1, source_target_pairs={{0,16},{16,0},{32,48},{48,32},{64,80},{80,64},{96,112},{112,96},{1... | collective-permute-start | bytes 2457608 | tf_op jit(solution)/shard_map/cond/branch_0_fun/ppermute | solution.py:20
  352.9 15.0 %collective-permute-start.1 = (bf16[1]{0:T(256)(128)(2,1)}, bf16[1]{0:T(256)(128)(2,1)}, u32[]{:S(2)}, u32[]{:S(2)}) collective-permute-start(bf16[1]{0:T(256)(128)(2,1)} %convert_element_type.74), channel_id=1, source_target_pairs={{0,16},{16,0},{32,48},{48,32},{64,80},{80,64},{96,112},{112,96},{1... | collective-permute-start | bytes 14 | tf_op jit(solution)/shard_map/cond/branch_0_fun/ppermute | solution.py:20
Sparse Core Ops, SparseCore 0:
  11.1 146.5 all-gather.1
  195.7 154.1 reduce-scatter.1

commit v2 on v1

--- a/solution.py
+++ b/solution.py
@@ -21,23 +21,25 @@
 
 
 def on_device(attn, resid, cotangent, gain, numer, pweight, round_bit):
-    n_sh = lax.axis_size("sh")
+    n_zh = lax.axis_size("zh")
+    n_y = lax.axis_size("y")
     n_core = lax.axis_size("core")
     acts = attn[0]
     tok, din = acts.shape
-    rows = din // (n_sh * n_core)
+    rows = din // (n_zh * n_y * n_core)
     weight_rows = (numer[0] / pweight[0]).astype(jnp.bfloat16)
     me = lax.axis_index("core")
     other = [(i, i ^ 1) for i in range(n_core)]
-    w_own = lax.all_gather(weight_rows, "sh", axis=0, tiled=False)
+    w_z = lax.all_gather(weight_rows, "zh", axis=0, tiled=False)
+    w_own = lax.all_gather(w_z, "y", axis=0, tiled=False)
     w_other = lax.ppermute(w_own, "core", other)
-    acts4 = acts.reshape(tok, n_sh, n_core, rows)
-    a_own = lax.dynamic_index_in_dim(acts4, me, axis=2, keepdims=False)
-    a_other = lax.dynamic_index_in_dim(acts4, 1 - me, axis=2, keepdims=False)
+    acts5 = acts.reshape(tok, n_zh, n_y, n_core, rows)
+    a_own = lax.dynamic_index_in_dim(acts5, me, axis=3, keepdims=False)
+    a_other = lax.dynamic_index_in_dim(acts5, 1 - me, axis=3, keepdims=False)
     pre = (
         resid[0].astype(jnp.float32)
-        + jnp.einsum("tsi,sio->to", a_own, w_own, preferred_element_type=jnp.float32)
-        + jnp.einsum("tsi,sio->to", a_other, w_other, preferred_element_type=jnp.float32)
+        + jnp.einsum("tzyi,yzio->to", a_own, w_own, preferred_element_type=jnp.float32)
+        + jnp.einsum("tzyi,yzio->to", a_other, w_other, preferred_element_type=jnp.float32)
     )
     inv = lax.rsqrt(jnp.mean(pre * pre, axis=1, keepdims=True) + EPS)
     normed = pre * inv
@@ -46,13 +48,16 @@
         jnp.bfloat16
     )
     part_other = jnp.einsum(
-        "tsi,to->sio", a_other, dpre, preferred_element_type=jnp.float32
+        "tzyi,to->yzio", a_other, dpre, preferred_element_type=jnp.float32
     ).astype(jnp.bfloat16)
     part_own = jnp.einsum(
-        "tsi,to->sio", a_own, dpre, preferred_element_type=jnp.float32
+        "tzyi,to->yzio", a_own, dpre, preferred_element_type=jnp.float32
     ).astype(jnp.bfloat16)
     part = part_own + lax.ppermute(part_other, "core", other)
-    grad = lax.psum_scatter(part, "sh", scatter_dimension=0, tiled=False).astype(jnp.float32)
+    part = part.reshape(n_y, n_zh * rows, part.shape[-1])
+    part = lax.psum_scatter(part, "y", scatter_dimension=0, tiled=False)
+    part = part.reshape(n_zh, rows, part.shape[-1])
+    grad = lax.psum_scatter(part, "zh", scatter_dimension=0, tiled=False).astype(jnp.float32)
     stepped = numer[0] - learning_rate * grad
     levels = lax.axis_size("rep").bit_length() - 1
 
@@ -77,9 +82,9 @@
 
 def solution(mesh):
     n_rep, n_shard = mesh.devices.shape
-    devices = np.asarray(mesh.devices).reshape(n_rep, n_shard // 2, 2)
-    split = Mesh(devices, ("rep", "sh", "core"))
-    rows = P("rep", ("sh", "core"), None)
+    devices = np.asarray(mesh.devices).reshape(n_rep, 2, n_shard // 4, 2)
+    split = Mesh(devices, ("rep", "zh", "y", "core"))
+    rows = P("rep", ("zh", "y", "core"), None)
     in_specs = (rows, rows, rows, P(), rows, P("rep"), P())
     out_specs = (rows, P("rep"))
     return jax.shard_map(

time: 381 us -> 342 us (0.90)
  waiting for transfers between devices: 314 us -> 259 us
  other arithmetic: 7.16 us -> 15.8 us
  local copies, waits for them, and re-layouts: 2.85 us -> 7.52 us
    reduce_scatter x1 -> x2, waiting for transfers between devices: 154 us -> 125 us  [the longest x1 69.3 us: on_device(): part = lax.psum_scatter(part, 'y', scatter_dimension=0, tiled=False)]
    all_gather x1 -> x2, waiting for transfers between devices: 147 us -> 126 us  [the longest x1 68.3 us: on_device(): w_own = lax.all_gather(w_z, 'y', axis=0, tiled=False)]
    unnamed x0 -> x2, matrix products: none -> 13.1 us
    dot_general x4 -> x2, matrix products: 20.7 us -> 10.3 us  [the longest x1 5.33 us: on_device(): jnp.einsum('tzyi,yzio->to', a_other, w_other, preferred_element_type=jnp....]
    convert_element_type x1, other arithmetic: 1.03 us -> 8.19 us  [on_device(): part_other = jnp.einsum('tzyi,to->yzio', a_other, dpre, preferred_element...]
    ppermute x1, waiting for transfers between devices: 10.4 us -> 4.68 us  [on_device(): part = part_own + lax.ppermute(part_other, 'core', other)]
  transfers between devices with their start and end apart: 6 -> 8, of which waited for: 5 -> 7; matrix products, arithmetic and copies ran while one was open for 2% -> 4% of each run, Pallas kernels for 0% -> 0%
where the time goes in v2:
time: 342 us; the launch traced here: 341 us
  waiting for transfers between devices  259 us (76%)
  matrix products  23.4 us (7%)
  starting transfers between devices  17.8 us (5%)
  between operations  16.3 us (5%)
  other arithmetic  15.8 us (5%)
  local copies, waits for them, and re-layouts  7.52 us (2%)
    reduce_scatter x1, waiting for transfers between devices, on_device(): part = lax.psum_scatter(part, 'y', scatter_dimension=0, tiled=False)  69.3 us
    all_gather x1, waiting for transfers between devices, on_device(): w_own = lax.all_gather(w_z, 'y', axis=0, tiled=False)  68.3 us
    all_gather x1, waiting for transfers between devices, on_device(): w_z = lax.all_gather(weight_rows, 'zh', axis=0, tiled=False)  58 us
    reduce_scatter x1, waiting for transfers between devices, on_device(): lax.psum_scatter(part, 'zh', scatter_dimension=0, tiled=False)  55.4 us
    ppermute x2, starting transfers between devices, from_partner(): lax.ppermute(shard, axis, [(i, i ^ 1 << apart) for i in range(lax.axis_si...  17.3 us
    unnamed x2, matrix products  13.1 us
    convert_element_type x1, other arithmetic, on_device(): part_other = jnp.einsum('tzyi,to->yzio', a_other, dpre, preferred_element...  8.19 us
  transfers between devices with their start and end apart: 8, of which 7 were waited for; matrix products, arithmetic and copies ran while one was open for 4% of the time, Pallas kernels for 0%

profile of v2, /device:TPU:2, one launch (start us, length us, event | category | flops | bytes accessed | tf_op | source)
XLA Modules:
  0.0 341.4 jit_solution(16788348450064306390)
XLA Ops:
  7.9 2.4 divide_convert_fusion
  10.3 58.0 %all-gather.4.cloned.1.call-done = bf16[2,160,2560]{2,1,0:T(8,128)(2,1)} async-done(((bf16[1,160,2560]{2,1,0:T(8,128)(2,1)}), bf16[2,160,2560]{2,1,0:T(8,128)(2,1)}) %all-gather.4.cloned.1.call-update) | async-done | bytes 1638416 | tf_op jit(solution)/shard_map/all_gather | solution.py:33
  68.5 68.3 %all-gather.6.cloned.1.call-done = bf16[8,160,2560]{2,1,0:T(8,128)(2,1)} async-done(((bf16[2,160,2560]{2,1,0:T(8,128)(2,1)}), bf16[8,160,2560]{2,1,0:T(8,128)(2,1)}) %all-gather.6.cloned.1.call-update) | async-done | bytes 6553616 | tf_op jit(solution)/shard_map/all_gather | solution.py:34
  136.7 2.8 copy.19
  139.6 0.3 constant_dynamic-slice_fusion.1
  139.9 1.3 copy-done.3
  141.1 5.0 %fusion = f32[384,2560]{1,0:T(8,128)S(1)} fusion(bf16[4,2,160,2560]{3,2,1,0:T(8,128)(2,1)} %bitcast.63, bf16[1,384,2560]{2,1,0:T(8,128)(2,1)S(1)} %copy-done.3, bf16[384,2,4,1,160]{0,4,3,2,1:T(8,128)(2,1)S(1)} %get-tuple-element.48), kind=kOutput, calls=%fused_computation.4 | convolution fusion | flops 2518548480 | bytes 13434880 | tf_op jit(solution)/shard_map/tzyi,yzio->to/dot_general | solution.py:41
  146.1 1.5 collective-permute-done.8
  147.6 5.3 %multiply_reduce_fusion = (f32[384]{0:T(512)S(1)}, f32[384,2560]{1,0:T(8,128)S(1)}) fusion(f32[384,2560]{1,0:T(8,128)S(1)} %fusion, bf16[4,2,160,2560]{3,2,1,0:T(8,128)(2,1)} %collective-permute-done.8, bf16[384,2,4,1,160]{0,4,3,2,1:T(8,128)(2,1)S(1)} %get-tuple-element.49), kind=kOutput, calls=%fused_computation.12 | convolution fusion | flops 2519531008 | bytes 15402496 | tf_op jit(solution)/shard_map/tzyi,yzio->to/dot_general | solution.py:42
  153.0 0.8 fusion.4
  153.8 7.2 %fusion.13 = f32[2560,1280]{0,1} fusion(bf16[384,1280]{0,1:T(8,128)(2,1)S(1)} %bitcast.60, f32[384,2560]{1,0:T(8,128)S(1)} %get-tuple-element.51, bf16[1,384,2560]{2,1,0:T(8,128)(2,1)S(1)} %copy-done.1, f32[384]{0:T(512)S(1)} %broadcast_multiply_fusion, f32[2560]{0:T(1024)S(1)} %copy-done.4, f32[384]{0:T(512)S(1)} %add_rsqrt_fusion), kind=kOutput, calls=%fused_computation.25 | convolution fusion | flops 2523463680 | bytes 20001792
  161.0 8.2 %convert_bitcast_fusion = bf16[4,2,160,2560]{3,2,0,1:T(8,128)(2,1)} fusion(f32[2560,2,4,160]{0,3,2,1:T(8,128)} %bitcast.57), kind=kLoop, calls=%fused_computation.1 | loop fusion | flops 3276800 | bytes 19660800 | tf_op jit(solution)/shard_map/convert_element_type | solution.py:52
  169.3 5.9 %fusion.11 = f32[2560,1280]{0,1:S(1)} fusion(bf16[384,1280]{0,1:T(8,128)(2,1)S(1)} %bitcast.59, f32[384,2560]{1,0:T(8,128)} %copy-done, bf16[1,384,2560]{2,1,0:T(8,128)(2,1)S(1)} %copy-done.1, f32[384]{0:T(512)S(1)} %broadcast_multiply_fusion, f32[2560]{0:T(1024)S(1)} %copy-done.4, f32[384]{0:T(512)S(1)} %add_rsqrt_fusion), kind=kOutput, calls=%fused_computation.24 | convolution fusion | flops 2523463680 | bytes 20001792
  175.2 4.7 %collective-permute-done.9 = bf16[4,2,160,2560]{3,2,0,1:T(8,128)(2,1)S(1)} collective-permute-done((bf16[4,2,160,2560]{3,2,0,1:T(8,128)(2,1)}, bf16[4,2,160,2560]{3,2,0,1:T(8,128)(2,1)S(1)}, u32[]{:S(2)}, u32[]{:S(2)}) %collective-permute-start.9) | collective-permute-done | bytes 6553632 | tf_op jit(solution)/shard_map/ppermute | solution.py:56
  179.9 1.4 bitcast_add_fusion
  181.3 3.1 copy.24
  184.7 69.3 %reduce-scatter.3.cloned.1.call-done = bf16[1,320,2560]{2,1,0:T(8,128)(2,1)} async-done(((bf16[4,320,2560]{2,1,0:T(8,128)(2,1)}), bf16[1,320,2560]{2,1,0:T(8,128)(2,1)}) %reduce-scatter.3.cloned.1.call-update) | async-done | bytes 1638416 | tf_op jit(solution)/shard_map/reduce_scatter | solution.py:58
  254.7 55.4 %reduce-scatter.5.cloned.1.call-done = bf16[1,160,2560]{2,1,0:T(8,128)(2,1)} async-done(((bf16[2,160,2560]{2,1,0:T(8,128)(2,1)}), bf16[1,160,2560]{2,1,0:T(8,128)(2,1)}) %reduce-scatter.5.cloned.1.call-update) | async-done | bytes 819216 | tf_op jit(solution)/shard_map/reduce_scatter | solution.py:60
  310.1 1.3 subtract_bitcast_fusion
  311.4 20.9 %conditional.4 = (f32[160,2560]{1,0:T(8,128)S(1)}, f32[1]{0:T(128)}) conditional(s32[]{:T(128)} %bitcast.22, (f32[160,2560]{1,0:T(8,128)S(1)}, f32[1]{0:T(128)}) %tuple.50, (f32[160,2560]{1,0:T(8,128)S(1)}, f32[1]{0:T(128)}) %tuple.50, (f32[160,2560]{1,0:T(8,128)S(1)}, f32[1]{0:T(128)}) %tuple.50, ...), branch_computations={%region_4.5_spmd, %region_5.6_spmd, %region_6.7_spmd, %region_7.8_... | conditional | flops 819202 | bytes 8192116
  311.6 0.6 collective-permute-start
  312.8 16.7 %collective-permute-start.1 = (bf16[1]{0:T(256)(128)(2,1)}, bf16[1]{0:T(256)(128)(2,1)}, u32[]{:S(2)}, u32[]{:S(2)}) collective-permute-start(bf16[1]{0:T(256)(128)(2,1)} %convert_element_type.78), channel_id=1, source_target_pairs={{0,16},{16,0},{32,48},{48,32},{64,80},{80,64},{96,112},{112,96},{1... | collective-permute-start | bytes 14 | tf_op jit(solution)/shard_map/cond/branch_0_fun/ppermute | solution.py:20
  329.6 1.9 collective-permute-done.1
  332.4 1.3 multiply_bitcast_fusion
  (24 shorter events, 0.8 us)
Async XLA Ops:
  7.2 61.2 %all-gather.4.cloned.1.call-start = ((), (), s32[]{:S(2)}) async-start(), calls=%async_computation.2 | async-start | bytes 2457600 | tf_op jit(solution)/shard_map/all_gather | solution.py:33
  10.3 126.4 %all-gather.6.cloned.1.call-start = ((), (), s32[]{:S(2)}) async-start(), calls=%async_computation.5 | async-start | bytes 8192000 | tf_op jit(solution)/shard_map/all_gather | solution.py:34
  68.4 185.6 %reduce-scatter.3.cloned.1.call-start = ((), (), s32[]{:S(2)}) async-start(), calls=%async_computation.3 | async-start | bytes 8192000 | tf_op jit(solution)/shard_map/reduce_scatter | solution.py:58
  136.7 10.9 %collective-permute-start.8 = (bf16[4,2,160,2560]{3,2,1,0:T(8,128)(2,1)}, bf16[4,2,160,2560]{3,2,1,0:T(8,128)(2,1)}, u32[]{:S(2)}, u32[]{:S(2)}) collective-permute-start(bf16[4,2,160,2560]{3,2,1,0:T(8,128)(2,1)} %bitcast.62), channel_id=1, source_target_pairs={{0,1},{1,0},{2,3},{3,2},{4,5},{5,4},{6,7},{7,6},{8,9},{9,8},{10,11... | collective-permute-start | bytes 19660808 | tf_op jit(solution)/shard_map/ppermute | solution.py:35
  139.6 1.5 copy-start.3
  147.6 5.4 %copy-start.1 = (bf16[1,384,2560]{2,1,0:T(8,128)(2,1)S(1)}, bf16[1,384,2560]{2,1,0:T(8,128)(2,1)}, u32[]{:S(2)}) copy-start(bf16[1,384,2560]{2,1,0:T(8,128)(2,1)} %param.13) | copy-start | bytes 5898244
  147.6 5.4 %copy-start.4 = (f32[2560]{0:T(1024)S(1)}, f32[2560]{0:T(1024)}, u32[]{:S(2)}) copy-start(f32[2560]{0:T(1024)} %param.14) | copy-start | bytes 30724
  152.9 8.0 %copy-start = (f32[384,2560]{1,0:T(8,128)}, f32[384,2560]{1,0:T(8,128)S(1)}, u32[]{:S(2)}) copy-start(f32[384,2560]{1,0:T(8,128)S(1)} %get-tuple-element.51) | copy-start | bytes 11796484
  169.2 10.7 %collective-permute-start.9 = (bf16[4,2,160,2560]{3,2,0,1:T(8,128)(2,1)}, bf16[4,2,160,2560]{3,2,0,1:T(8,128)(2,1)S(1)}, u32[]{:S(2)}, u32[]{:S(2)}) collective-permute-start(bf16[4,2,160,2560]{3,2,0,1:T(8,128)(2,1)} %convert_bitcast_fusion), channel_id=1, source_target_pairs={{0,1},{1,0},{2,3},{3,2},{4,5},{5,4},{6,7},{7,6},{8,9},{9,8},{10,11... | collective-permute-start | bytes 19660808 | tf_op jit(solution)/shard_map/ppermute | solution.py:56
  184.5 125.6 %copy-start.2 = (f32[1,160,2560]{2,1,0:T(8,128)S(1)}, f32[1,160,2560]{2,1,0:T(8,128)}, u32[]{:S(2)}) copy-start(f32[1,160,2560]{2,1,0:T(8,128)} %param.15) | copy-start | bytes 4915204
  184.5 125.6 %reduce-scatter.5.cloned.1.call-start = ((), (), s32[]{:S(2)}) async-start(), calls=%async_computation.4 | async-start | bytes 2457600 | tf_op jit(solution)/shard_map/reduce_scatter | solution.py:60
  311.6 20.6 %collective-permute-start = (bf16[160,2560]{1,0:T(8,128)(2,1)S(1)}, bf16[160,2560]{1,0:T(8,128)(2,1)S(1)}, u32[]{:S(2)}, u32[]{:S(2)}) collective-permute-start(bf16[160,2560]{1,0:T(8,128)(2,1)S(1)} %convert_element_type.76), channel_id=1, source_target_pairs={{0,16},{16,0},{32,48},{48,32},{64,80},{80,64},{96,112},{112,96},{1... | collective-permute-start | bytes 2457608 | tf_op jit(solution)/shard_map/cond/branch_0_fun/ppermute | solution.py:20
  312.8 18.6 %collective-permute-start.1 = (bf16[1]{0:T(256)(128)(2,1)}, bf16[1]{0:T(256)(128)(2,1)}, u32[]{:S(2)}, u32[]{:S(2)}) collective-permute-start(bf16[1]{0:T(256)(128)(2,1)} %convert_element_type.78), channel_id=1, source_target_pairs={{0,16},{16,0},{32,48},{48,32},{64,80},{80,64},{96,112},{112,96},{1... | collective-permute-start | bytes 14 | tf_op jit(solution)/shard_map/cond/branch_0_fun/ppermute | solution.py:20
Sparse Core Ops, SparseCore 0:
  10.4 57.9 all-gather.3
  70.2 66.4 all-gather.5
  184.6 69.3 reduce-scatter.2
  256.4 53.6 reduce-scatter.4

commit v3 on v2

--- a/solution.py
+++ b/solution.py
@@ -28,18 +28,31 @@
     tok, din = acts.shape
     rows = din // (n_zh * n_y * n_core)
     weight_rows = (numer[0] / pweight[0]).astype(jnp.bfloat16)
-    me = lax.axis_index("core")
-    other = [(i, i ^ 1) for i in range(n_core)]
-    w_z = lax.all_gather(weight_rows, "zh", axis=0, tiled=False)
-    w_own = lax.all_gather(w_z, "y", axis=0, tiled=False)
-    w_other = lax.ppermute(w_own, "core", other)
+    me_c = lax.axis_index("core")
+    me_z = lax.axis_index("zh")
+    swap_core = [(i, i ^ 1) for i in range(n_core)]
+    swap_z = [(i, i ^ 1) for i in range(n_zh)]
     acts5 = acts.reshape(tok, n_zh, n_y, n_core, rows)
-    a_own = lax.dynamic_index_in_dim(acts5, me, axis=3, keepdims=False)
-    a_other = lax.dynamic_index_in_dim(acts5, 1 - me, axis=3, keepdims=False)
+
+    def cols(z, c):
+        near = lax.dynamic_index_in_dim(acts5, z, axis=1, keepdims=False)
+        return lax.dynamic_index_in_dim(near, c, axis=2, keepdims=False)
+
+    w_near = lax.all_gather(weight_rows, "y", axis=0, tiled=False)
+    w_near, w_cross = lax.optimization_barrier((w_near, lax.ppermute(weight_rows, "zh", swap_z)))
+    w_far = lax.all_gather(w_cross, "y", axis=0, tiled=False)
+    w_near_o = lax.ppermute(w_near, "core", swap_core)
+    w_far_o = lax.ppermute(w_far, "core", swap_core)
+
+    def mm(a, w):
+        return jnp.einsum("tyi,yio->to", a, w, preferred_element_type=jnp.float32)
+
     pre = (
         resid[0].astype(jnp.float32)
-        + jnp.einsum("tzyi,yzio->to", a_own, w_own, preferred_element_type=jnp.float32)
-        + jnp.einsum("tzyi,yzio->to", a_other, w_other, preferred_element_type=jnp.float32)
+        + mm(cols(me_z, me_c), w_near)
+        + mm(cols(me_z, 1 - me_c), w_near_o)
+        + mm(cols(1 - me_z, me_c), w_far)
+        + mm(cols(1 - me_z, 1 - me_c), w_far_o)
     )
     inv = lax.rsqrt(jnp.mean(pre * pre, axis=1, keepdims=True) + EPS)
     normed = pre * inv
@@ -47,17 +60,17 @@
     dpre = (inv * (dnorm - normed * jnp.mean(dnorm * normed, axis=1, keepdims=True))).astype(
         jnp.bfloat16
     )
-    part_other = jnp.einsum(
-        "tzyi,to->yzio", a_other, dpre, preferred_element_type=jnp.float32
-    ).astype(jnp.bfloat16)
-    part_own = jnp.einsum(
-        "tzyi,to->yzio", a_own, dpre, preferred_element_type=jnp.float32
-    ).astype(jnp.bfloat16)
-    part = part_own + lax.ppermute(part_other, "core", other)
-    part = part.reshape(n_y, n_zh * rows, part.shape[-1])
-    part = lax.psum_scatter(part, "y", scatter_dimension=0, tiled=False)
-    part = part.reshape(n_zh, rows, part.shape[-1])
-    grad = lax.psum_scatter(part, "zh", scatter_dimension=0, tiled=False).astype(jnp.float32)
+
+    def tm(a):
+        return jnp.einsum("tyi,to->yio", a, dpre, preferred_element_type=jnp.float32).astype(
+            jnp.bfloat16
+        )
+
+    far = tm(cols(1 - me_z, me_c)) + lax.ppermute(tm(cols(1 - me_z, 1 - me_c)), "core", swap_core)
+    far = lax.ppermute(lax.psum_scatter(far, "y", scatter_dimension=0, tiled=False), "zh", swap_z)
+    near = tm(cols(me_z, me_c)) + lax.ppermute(tm(cols(me_z, 1 - me_c)), "core", swap_core)
+    near = lax.psum_scatter(near, "y", scatter_dimension=0, tiled=False)
+    grad = near.astype(jnp.float32) + far.astype(jnp.float32)
     stepped = numer[0] - learning_rate * grad
     levels = lax.axis_size("rep").bit_length() - 1
 

time: 342 us -> 251 us (0.73)
  waiting for transfers between devices: 259 us -> 162 us
  starting transfers between devices: 17.8 us -> 33 us
  other arithmetic: 15.8 us -> 7.58 us
  local copies, waits for them, and re-layouts: 7.52 us -> 4.1 us
    all_gather x2, waiting for transfers between devices: 126 us -> 49.9 us  [the longest x1 45.6 us: on_device(): w_far = lax.all_gather(w_cross, 'y', axis=0, tiled=False)]
    reduce_scatter x2, waiting for transfers between devices: 125 us -> 65.7 us  [the longest x1 37.7 us: on_device(): near = lax.psum_scatter(near, 'y', scatter_dimension=0, tiled=False)]
    ppermute x2 -> x6, waiting for transfers between devices: 6.19 us -> 45.4 us  [the longest x1 34.5 us: on_device(): lax.ppermute(weight_rows, 'zh', swap_z)]
    dot_general x2 -> x8, matrix products: 10.3 us -> 25.9 us  [the longest x4 13.8 us: tm(): jnp.einsum('tyi,to->yio', a, dpre, preferred_element_type=jnp.float32)]
    ppermute x2 -> x6, starting transfers between devices: 0.15 us -> 14.3 us  [the longest x1 7.28 us: on_device(): lax.ppermute(weight_rows, 'zh', swap_z)]
    unnamed x2 -> x0, matrix products: 13.1 us -> none
    convert_element_type x1, other arithmetic: 8.19 us -> 1.04 us  [on_device(): (inv * (dnorm - normed * jnp.mean(dnorm * normed, axis=1, keepdims=True))...]
  transfers between devices with their start and end apart: 8 -> 12, of which waited for: 7 -> 8; matrix products, arithmetic and copies ran while one was open for 4% -> 7% of each run, Pallas kernels for 0% -> 0%
where the time goes in v3:
time: 251 us; the launch traced here: 250 us
  waiting for transfers between devices  162 us (65%)
  starting transfers between devices  33 us (13%)
  matrix products  25.9 us (10%)
  between operations  16.5 us (7%)
  other arithmetic  7.58 us (3%)
  local copies, waits for them, and re-layouts  4.1 us (2%)
    all_gather x1, waiting for transfers between devices, on_device(): w_far = lax.all_gather(w_cross, 'y', axis=0, tiled=False)  45.6 us
    reduce_scatter x1, waiting for transfers between devices, on_device(): near = lax.psum_scatter(near, 'y', scatter_dimension=0, tiled=False)  37.7 us
    ppermute x1, waiting for transfers between devices, on_device(): lax.ppermute(weight_rows, 'zh', swap_z)  34.5 us
    reduce_scatter x1, waiting for transfers between devices, on_device(): lax.psum_scatter(far, 'y', scatter_dimension=0, tiled=False)  28 us
    ppermute x2, starting transfers between devices, from_partner(): lax.ppermute(shard, axis, [(i, i ^ 1 << apart) for i in range(lax.axis_si...  18.5 us
    dot_general x4, matrix products, tm(): jnp.einsum('tyi,to->yio', a, dpre, preferred_element_type=jnp.float32)  13.8 us
    dot_general x4, matrix products, mm(): return jnp.einsum('tyi,yio->to', a, w, preferred_element_type=jnp.float32)  12.1 us
    ppermute x1, starting transfers between devices, on_device(): lax.ppermute(weight_rows, 'zh', swap_z)  7.28 us
  transfers between devices with their start and end apart: 12, of which 8 were waited for; matrix products, arithmetic and copies ran while one was open for 7% of the time, Pallas kernels for 0%

profile of v3, /device:TPU:2, one launch (start us, length us, event | category | flops | bytes accessed | tf_op | source)
XLA Modules:
  0.0 250.5 jit_solution(8070553268963697296)
XLA Ops:
  8.0 2.4 divide_convert_fusion
  10.6 7.3 %collective-permute-start.8 = (bf16[160,2560]{1,0:T(8,128)(2,1)S(1)}, bf16[160,2560]{1,0:T(8,128)(2,1)S(1)}, u32[]{:S(2)}, u32[]{:S(2)}) collective-permute-start(bf16[160,2560]{1,0:T(8,128)(2,1)S(1)} %fusion.14), channel_id=1, source_target_pairs={{0,8},{8,0},{1,9},{9,1},{2,10},{10,2},{3,11},{11,3},{4,12},{12,4},... | collective-permute-start | bytes 2457608 | tf_op jit(solution)/shard_map/ppermute | solution.py:42
  17.9 34.5 %collective-permute-done.8 = bf16[160,2560]{1,0:T(8,128)(2,1)S(1)} collective-permute-done((bf16[160,2560]{1,0:T(8,128)(2,1)S(1)}, bf16[160,2560]{1,0:T(8,128)(2,1)S(1)}, u32[]{:S(2)}, u32[]{:S(2)}) %collective-permute-start.8) | collective-permute-done | bytes 819232 | tf_op jit(solution)/shard_map/ppermute | solution.py:42
  52.3 4.3 %all-gather.4.cloned.1.call-done = bf16[4,160,2560]{2,1,0:T(8,128)(2,1)} async-done(((bf16[1,160,2560]{2,1,0:T(8,128)(2,1)}), bf16[4,160,2560]{2,1,0:T(8,128)(2,1)}) %all-gather.4.cloned.1.call-update) | async-done | bytes 3276816 | tf_op jit(solution)/shard_map/all_gather | solution.py:41
  56.9 45.6 %all-gather.6.cloned.1.call-done = bf16[640,2560]{1,0:T(8,128)(2,1)} async-done(((bf16[160,2560]{1,0:T(8,128)(2,1)}), bf16[640,2560]{1,0:T(8,128)(2,1)}) %all-gather.6.cloned.1.call-update) | async-done | bytes 3276816 | tf_op jit(solution)/shard_map/all_gather | solution.py:43
  102.5 4.0 %copy.14 = bf16[1,384,2560]{1,2,0:T(8,128)(2,1)} copy(bf16[1,384,2560]{2,1,0:T(8,128)(2,1)} %param.11) | data formatting | bytes 3932160 | tf_op args[0]
  106.5 4.0 %convolution_bitcast_fusion.2 = f32[384,2560]{1,0:T(8,128)S(1)} fusion(bf16[4,160,2560]{2,1,0:T(8,128)(2,1)} %collective-permute-done.9, bf16[384,2,4,2,160]{0,4,3,2,1:T(8,128)(2,1)} %bitcast.72, s32[]{:T(128)S(6)} %select_n.35, s32[]{:T(128)S(6)} %select_n.39), kind=kOutput, calls=%fused_computation.6 | convolution fusion | flops 1258291200 | bytes 7700488 | tf_op jit(solution)/shard_map/tyi,yio->to/dot_general | solution.py:48
  110.5 1.7 convolution_bitcast_fusion.1
  112.3 3.8 %convolution_bitcast_fusion = f32[384,2560]{1,0:T(8,128)S(1)} fusion(bf16[4,160,2560]{2,1,0:T(8,128)(2,1)} %collective-permute-done.10, bf16[384,2,4,2,160]{0,4,3,2,1:T(8,128)(2,1)S(1)} %bitcast.76, s32[]{:T(128)S(6)} %select_n.41, s32[]{:T(128)S(6)} %select_n.39), kind=kOutput, calls=%fused_computation.4 | convolution fusion | flops 1258291200 | bytes 7700488 | tf_op jit(solution)/shard_map/tyi,yio->to/dot_general | solution.py:48
  116.1 2.6 %multiply_reduce_fusion = (f32[384]{0:T(512)S(1)}, f32[384,2560]{1,0:T(8,128)S(1)}) fusion(f32[384,2560]{1,0:T(8,128)S(1)} %convolution_bitcast_fusion, f32[384,2560]{1,0:T(8,128)S(1)} %convolution_bitcast_fusion.1, f32[384,2560]{1,0:T(8,128)S(1)} %convolution_bitcast_fusion.2, bf16[4,160,2560]{2,1,0:T(8,128)(2,1)S(1)} %copy-done.4, ...), kind=kOutput, calls=%fused_computation.20 | convolution fusion | flops 1265172096 | bytes 21464584 | tf_op jit(solution)/shard_map/tyi,yio->to/dot_general | solution.py:48
  120.6 1.9 convolution_convert_fusion
  123.3 5.5 %collective-permute-done.12 = bf16[4,160,2560]{2,1,0:T(8,128)(2,1)S(1)} collective-permute-done((bf16[4,160,2560]{2,1,0:T(8,128)(2,1)S(1)}, bf16[4,160,2560]{2,1,0:T(8,128)(2,1)S(1)}, u32[]{:S(2)}, u32[]{:S(2)}) %collective-permute-start.12) | collective-permute-done | bytes 3276832 | tf_op jit(solution)/shard_map/ppermute | solution.py:69
  128.7 3.6 %fusion.5 = bf16[4,160,2560]{2,1,0:T(8,128)(2,1)} fusion(bf16[4,160,2560]{2,1,0:T(8,128)(2,1)S(1)} %collective-permute-done.12, bf16[384,2560,1]{1,0,2:T(8,128)(2,1)S(1)} %fusion.11, bf16[384,2,4,2,160]{0,4,3,2,1:T(8,128)(2,1)S(1)} %bitcast.79, s32[]{:T(128)S(6)} %select_n.41, s32[]{:T(128)S(6)} %select_n.37), kind=kOutput, calls=%fused_computation.13 | convolution fusion | flops 1261568000 | bytes 9011208 | tf_op jit(solution)/shard_map/tyi,to->yio/dot_general | solution.py:65
  132.4 3.7 %convolution_convert_fusion.2 = bf16[4,160,2560]{2,1,0:T(8,128)(2,1)S(1)} fusion(bf16[384,2560,1]{1,0,2:T(8,128)(2,1)} %copy-done.6, bf16[384,2,4,2,160]{0,4,3,2,1:T(8,128)(2,1)} %bitcast.73, s32[]{:T(128)S(6)} %select_n.35, s32[]{:T(128)S(6)} %select_n.39), kind=kOutput, calls=%fused_computation.2 | convolution fusion | flops 1259929600 | bytes 5734408 | tf_op jit(solution)/shard_map/tyi,to->yio/dot_general | solution.py:65
  136.5 5.5 %collective-permute-done.11 = bf16[4,160,2560]{2,1,0:T(8,128)(2,1)S(1)} collective-permute-done((bf16[4,160,2560]{2,1,0:T(8,128)(2,1)S(1)}, bf16[4,160,2560]{2,1,0:T(8,128)(2,1)S(1)}, u32[]{:S(2)}, u32[]{:S(2)}) %collective-permute-start.11) | collective-permute-done | bytes 3276832 | tf_op jit(solution)/shard_map/ppermute | solution.py:71
  142.0 4.6 %fusion.4 = bf16[4,160,2560]{2,1,0:T(8,128)(2,1)} fusion(bf16[4,160,2560]{2,1,0:T(8,128)(2,1)S(1)} %collective-permute-done.11, bf16[384,2560,1]{1,0,2:T(8,128)(2,1)S(1)} %copy-done.7, bf16[384,2,4,2,160]{0,4,3,2,1:T(8,128)(2,1)} %bitcast.74, s32[]{:T(128)S(6)} %select_n.35, s32[]{:T(128)S(6)} %select_n.37), kind=kOutput, calls=%fused_computation.12 | convolution fusion | flops 1261568000 | bytes 9011208 | tf_op jit(solution)/shard_map/tyi,to->yio/dot_general | solution.py:65
  146.7 28.0 %reduce-scatter.5.cloned.1.call-done = bf16[1,160,2560]{2,1,0:T(8,128)(2,1)} async-done(((bf16[4,160,2560]{2,1,0:T(8,128)(2,1)}), bf16[1,160,2560]{2,1,0:T(8,128)(2,1)}) %reduce-scatter.5.cloned.1.call-update) | async-done | bytes 819216 | tf_op jit(solution)/shard_map/reduce_scatter | solution.py:70
  174.6 5.7 %collective-permute-start.13 = (bf16[160,2560]{1,0:T(8,128)(2,1)}, bf16[160,2560]{1,0:T(8,128)(2,1)}, u32[]{:S(2)}, u32[]{:S(2)}) collective-permute-start(bf16[160,2560]{1,0:T(8,128)(2,1)} %bitcast.82), channel_id=1, source_target_pairs={{0,8},{8,0},{1,9},{9,1},{2,10},{10,2},{3,11},{11,3},{4,12},{12,4},... | collective-permute-start | bytes 2457608 | tf_op jit(solution)/shard_map/ppermute | solution.py:70
  181.0 37.7 %reduce-scatter.3.cloned.1.call-done = bf16[1,160,2560]{2,1,0:T(8,128)(2,1)} async-done(((bf16[4,160,2560]{2,1,0:T(8,128)(2,1)}), bf16[1,160,2560]{2,1,0:T(8,128)(2,1)}) %reduce-scatter.3.cloned.1.call-update) | async-done | bytes 819216 | tf_op jit(solution)/shard_map/reduce_scatter | solution.py:72
  218.7 1.7 fusion.13
  220.4 21.1 %conditional.4 = (f32[160,2560]{1,0:T(8,128)S(1)}, f32[1]{0:T(128)}) conditional(s32[]{:T(128)} %bitcast.17, (f32[160,2560]{1,0:T(8,128)S(1)}, f32[1]{0:T(128)}) %tuple.52, (f32[160,2560]{1,0:T(8,128)S(1)}, f32[1]{0:T(128)}) %tuple.52, (f32[160,2560]{1,0:T(8,128)S(1)}, f32[1]{0:T(128)}) %tuple.52, ...), branch_computations={%region_4.5_spmd, %region_5.6_spmd, %region_6.7_spmd, %region_7.8_... | conditional | flops 819202 | bytes 8192116
  220.5 1.7 collective-permute-start.4
  222.8 16.8 %collective-permute-start.5 = (bf16[1]{0:T(256)(128)(2,1)}, bf16[1]{0:T(256)(128)(2,1)}, u32[]{:S(2)}, u32[]{:S(2)}) collective-permute-start(bf16[1]{0:T(256)(128)(2,1)} %convert_element_type.90), channel_id=1, source_target_pairs={{0,64},{16,80},{32,96},{48,112},{64,0},{80,16},{96,32},{112,48},{1... | collective-permute-start | bytes 14 | tf_op jit(solution)/shard_map/cond/branch_2_fun/ppermute | solution.py:20
  241.5 1.3 multiply_bitcast_fusion
  (44 shorter events, 4.7 us)
Async XLA Ops:
  7.2 3.3 %copy-start = (f32[1,160,2560]{2,1,0:T(8,128)S(1)}, f32[1,160,2560]{2,1,0:T(8,128)}, u32[]{:S(2)}) copy-start(f32[1,160,2560]{2,1,0:T(8,128)} %param.15) | copy-start | bytes 4915204
  7.2 49.5 %all-gather.4.cloned.1.call-start = ((), (), s32[]{:S(2)}) async-start(), calls=%async_computation.2 | async-start | bytes 4096000 | tf_op jit(solution)/shard_map/all_gather | solution.py:41
  10.4 92.0 %all-gather.6.cloned.1.call-start = ((), (), s32[]{:S(2)}) async-start(), calls=%async_computation.5 | async-start | bytes 4096000 | tf_op jit(solution)/shard_map/all_gather | solution.py:43
  10.6 41.8 %collective-permute-start.8 = (bf16[160,2560]{1,0:T(8,128)(2,1)S(1)}, bf16[160,2560]{1,0:T(8,128)(2,1)S(1)}, u32[]{:S(2)}, u32[]{:S(2)}) collective-permute-start(bf16[160,2560]{1,0:T(8,128)(2,1)S(1)} %fusion.14), channel_id=1, source_target_pairs={{0,8},{8,0},{1,9},{9,1},{2,10},{10,2},{3,11},{11,3},{4,12},{12,4},... | collective-permute-start | bytes 2457608 | tf_op jit(solution)/shard_map/ppermute | solution.py:42
  52.3 4.3 %copy-start.8 = (bf16[160,2560]{1,0:T(8,128)(2,1)}, bf16[160,2560]{1,0:T(8,128)(2,1)S(1)}, u32[]{:S(2)}) copy-start(bf16[160,2560]{1,0:T(8,128)(2,1)S(1)} %collective-permute-done.8) | copy-start | bytes 2457604
  56.7 117.9 %reduce-scatter.5.cloned.1.call-start = ((), (), s32[]{:S(2)}) async-start(), calls=%async_computation.4 | async-start | bytes 4096000 | tf_op jit(solution)/shard_map/reduce_scatter | solution.py:70
  56.7 49.8 %collective-permute-start.9 = (bf16[4,160,2560]{2,1,0:T(8,128)(2,1)}, bf16[4,160,2560]{2,1,0:T(8,128)(2,1)}, u32[]{:S(2)}, u32[]{:S(2)}) collective-permute-start(bf16[4,160,2560]{2,1,0:T(8,128)(2,1)} %all-gather.4.cloned.1.call-done), channel_id=1, source_target_pairs={{0,1},{1,0},{2,3},{3,2},{4,5},{5,4},{6,7},{7,6},{8,9},{9,8},{10,11... | collective-permute-start | bytes 9830408 | tf_op jit(solution)/shard_map/ppermute | solution.py:44
  102.5 9.8 %collective-permute-start.10 = (bf16[4,160,2560]{2,1,0:T(8,128)(2,1)}, bf16[4,160,2560]{2,1,0:T(8,128)(2,1)}, u32[]{:S(2)}, u32[]{:S(2)}) collective-permute-start(bf16[4,160,2560]{2,1,0:T(8,128)(2,1)} %bitcast.80), channel_id=1, source_target_pairs={{0,1},{1,0},{2,3},{3,2},{4,5},{5,4},{6,7},{7,6},{8,9},{9,8},{10,11... | collective-permute-start | bytes 9830408 | tf_op jit(solution)/shard_map/ppermute | solution.py:45
  106.5 4.0 %copy-start.1 = (bf16[1,384,2560]{1,2,0:T(8,128)(2,1)S(1)}, bf16[1,384,2560]{1,2,0:T(8,128)(2,1)}, u32[]{:S(2)}) copy-start(bf16[1,384,2560]{1,2,0:T(8,128)(2,1)} %copy.14) | copy-start | bytes 5898244
  106.5 4.0 %copy-start.3 = (bf16[640,2560]{1,0:T(8,128)(2,1)S(1)}, bf16[640,2560]{1,0:T(8,128)(2,1)}, u32[]{:S(2)}) copy-start(bf16[640,2560]{1,0:T(8,128)(2,1)} %all-gather.6.cloned.1.call-done) | copy-start | bytes 9830404
  112.2 3.8 %copy-start.4 = (bf16[4,160,2560]{2,1,0:T(8,128)(2,1)S(1)}, bf16[4,160,2560]{2,1,0:T(8,128)(2,1)}, u32[]{:S(2)}) copy-start(bf16[4,160,2560]{2,1,0:T(8,128)(2,1)} %all-gather.4.cloned.1.call-done) | copy-start | bytes 9830404
  112.2 3.8 %copy-start.5 = (bf16[1,384,2560]{2,1,0:T(8,128)(2,1)S(1)}, bf16[1,384,2560]{2,1,0:T(8,128)(2,1)}, u32[]{:S(2)}) copy-start(bf16[1,384,2560]{2,1,0:T(8,128)(2,1)} %param.12) | copy-start | bytes 5898244
  116.1 2.7 %copy-start.2 = (bf16[1,384,2560]{2,1,0:T(8,128)(2,1)S(1)}, bf16[1,384,2560]{2,1,0:T(8,128)(2,1)}, u32[]{:S(2)}) copy-start(bf16[1,384,2560]{2,1,0:T(8,128)(2,1)} %param.13) | copy-start | bytes 5898244
  116.1 2.7 %copy-start.9 = (f32[2560]{0:T(1024)S(1)}, f32[2560]{0:T(1024)}, u32[]{:S(2)}) copy-start(f32[2560]{0:T(1024)} %param.14) | copy-start | bytes 30724
  120.6 8.1 %copy-start.6 = (bf16[384,2560,1]{1,0,2:T(8,128)(2,1)}, bf16[384,2560,1]{1,0,2:T(8,128)(2,1)S(1)}, u32[]{:S(2)}) copy-start(bf16[384,2560,1]{1,0,2:T(8,128)(2,1)S(1)} %fusion.11) | copy-start | bytes 5898244
  122.5 6.3 %collective-permute-start.12 = (bf16[4,160,2560]{2,1,0:T(8,128)(2,1)S(1)}, bf16[4,160,2560]{2,1,0:T(8,128)(2,1)S(1)}, u32[]{:S(2)}, u32[]{:S(2)}) collective-permute-start(bf16[4,160,2560]{2,1,0:T(8,128)(2,1)S(1)} %convolution_convert_fusion), channel_id=1, source_target_pairs={{0,1},{1,0},{2,3},{3,2},{4,5},{5,4},{6,7},{7,6},{8,9},{9,8},{10,11... | collective-permute-start | bytes 9830408 | tf_op jit(solution)/shard_map/ppermute | solution.py:69
  132.3 86.4 %reduce-scatter.3.cloned.1.call-start = ((), (), s32[]{:S(2)}) async-start(), calls=%async_computation.3 | async-start | bytes 4096000 | tf_op jit(solution)/shard_map/reduce_scatter | solution.py:72
  132.4 9.7 %copy-start.7 = (bf16[384,2560,1]{1,0,2:T(8,128)(2,1)S(1)}, bf16[384,2560,1]{1,0,2:T(8,128)(2,1)}, u32[]{:S(2)}) copy-start(bf16[384,2560,1]{1,0,2:T(8,128)(2,1)} %copy-done.6) | copy-start | bytes 5898244
  136.1 5.9 %collective-permute-start.11 = (bf16[4,160,2560]{2,1,0:T(8,128)(2,1)S(1)}, bf16[4,160,2560]{2,1,0:T(8,128)(2,1)S(1)}, u32[]{:S(2)}, u32[]{:S(2)}) collective-permute-start(bf16[4,160,2560]{2,1,0:T(8,128)(2,1)S(1)} %convolution_convert_fusion.2), channel_id=1, source_target_pairs={{0,1},{1,0},{2,3},{3,2},{4,5},{5,4},{6,7},{7,6},{8,9},{9,8},{10,11... | collective-permute-start | bytes 9830408 | tf_op jit(solution)/shard_map/ppermute | solution.py:71
  174.6 44.1 %collective-permute-start.13 = (bf16[160,2560]{1,0:T(8,128)(2,1)}, bf16[160,2560]{1,0:T(8,128)(2,1)}, u32[]{:S(2)}, u32[]{:S(2)}) collective-permute-start(bf16[160,2560]{1,0:T(8,128)(2,1)} %bitcast.82), channel_id=1, source_target_pairs={{0,8},{8,0},{1,9},{9,1},{2,10},{10,2},{3,11},{11,3},{4,12},{12,4},... | collective-permute-start | bytes 2457608 | tf_op jit(solution)/shard_map/ppermute | solution.py:70
  220.5 20.8 %collective-permute-start.4 = (bf16[160,2560]{1,0:T(8,128)(2,1)S(1)}, bf16[160,2560]{1,0:T(8,128)(2,1)S(1)}, u32[]{:S(2)}, u32[]{:S(2)}) collective-permute-start(bf16[160,2560]{1,0:T(8,128)(2,1)S(1)} %convert_element_type.88), channel_id=1, source_target_pairs={{0,64},{16,80},{32,96},{48,112},{64,0},{80,16},{96,32},{112,48},{1... | collective-permute-start | bytes 2457608 | tf_op jit(solution)/shard_map/cond/branch_2_fun/ppermute | solution.py:20
  222.8 17.8 %collective-permute-start.5 = (bf16[1]{0:T(256)(128)(2,1)}, bf16[1]{0:T(256)(128)(2,1)}, u32[]{:S(2)}, u32[]{:S(2)}) collective-permute-start(bf16[1]{0:T(256)(128)(2,1)} %convert_element_type.90), channel_id=1, source_target_pairs={{0,64},{16,80},{32,96},{48,112},{64,0},{80,16},{96,32},{112,48},{1... | collective-permute-start | bytes 14 | tf_op jit(solution)/shard_map/cond/branch_2_fun/ppermute | solution.py:20
Sparse Core Ops, SparseCore 0:
  10.5 46.0 all-gather.3
  59.1 43.3 all-gather.5
  132.4 42.1 reduce-scatter.4
  177.1 41.6 reduce-scatter.2

commit v4 on v3

--- a/solution.py
+++ b/solution.py
@@ -39,7 +39,11 @@
         return lax.dynamic_index_in_dim(near, c, axis=2, keepdims=False)
 
     w_near = lax.all_gather(weight_rows, "y", axis=0, tiled=False)
-    w_near, w_cross = lax.optimization_barrier((w_near, lax.ppermute(weight_rows, "zh", swap_z)))
+    a_nn, a_no = cols(me_z, me_c), cols(me_z, 1 - me_c)
+    a_fn, a_fo = cols(1 - me_z, me_c), cols(1 - me_z, 1 - me_c)
+    w_near, w_cross, a_nn, a_no, a_fn, a_fo = lax.optimization_barrier(
+        (w_near, lax.ppermute(weight_rows, "zh", swap_z), a_nn, a_no, a_fn, a_fo)
+    )
     w_far = lax.all_gather(w_cross, "y", axis=0, tiled=False)
     w_near_o = lax.ppermute(w_near, "core", swap_core)
     w_far_o = lax.ppermute(w_far, "core", swap_core)
@@ -47,13 +51,9 @@
     def mm(a, w):
         return jnp.einsum("tyi,yio->to", a, w, preferred_element_type=jnp.float32)
 
-    pre = (
-        resid[0].astype(jnp.float32)
-        + mm(cols(me_z, me_c), w_near)
-        + mm(cols(me_z, 1 - me_c), w_near_o)
-        + mm(cols(1 - me_z, me_c), w_far)
-        + mm(cols(1 - me_z, 1 - me_c), w_far_o)
-    )
+    pre_near = resid[0].astype(jnp.float32) + mm(a_nn, w_near)
+    pre_near = pre_near + mm(a_no, w_near_o)
+    pre = pre_near + mm(a_fn, w_far) + mm(a_fo, w_far_o)
     inv = lax.rsqrt(jnp.mean(pre * pre, axis=1, keepdims=True) + EPS)
     normed = pre * inv
     dnorm = cotangent[0].astype(jnp.float32) * gain
@@ -66,9 +66,14 @@
             jnp.bfloat16
         )
 
-    far = tm(cols(1 - me_z, me_c)) + lax.ppermute(tm(cols(1 - me_z, 1 - me_c)), "core", swap_core)
+    def own_plus_other(a_own, a_other):
+        sent = lax.ppermute(tm(a_other), "core", swap_core)
+        (own,) = lax.optimization_barrier((tm(a_own),))
+        return own + sent
+
+    far = own_plus_other(a_fn, a_fo)
     far = lax.ppermute(lax.psum_scatter(far, "y", scatter_dimension=0, tiled=False), "zh", swap_z)
-    near = tm(cols(me_z, me_c)) + lax.ppermute(tm(cols(me_z, 1 - me_c)), "core", swap_core)
+    near = own_plus_other(a_nn, a_no)
     near = lax.psum_scatter(near, "y", scatter_dimension=0, tiled=False)
     grad = near.astype(jnp.float32) + far.astype(jnp.float32)
     stepped = numer[0] - learning_rate * grad
@@ -76,20 +81,16 @@
 
     def pushed(bit):
 
-        def send_pair(pair):
-            return jax.tree.map(
-                lambda part, own: part.astype(own.dtype),
-                from_partner(shortened(pair), "rep", bit),
-                pair,
-            )
+        def send(part):
+            return from_partner(shortened(part), "rep", bit).astype(part.dtype)
 
-        return send_pair
+        return send
 
-    other_numer, other_weight = lax.switch(
-        round_bit[0], [pushed(level) for level in range(levels)], (stepped, pweight)
-    )
-    new_numer = (0.5 * (stepped + other_numer))[None]
-    new_pweight = 0.5 * (pweight + other_weight)
+    def gossip(part):
+        return lax.switch(round_bit[0], [pushed(level) for level in range(levels)], part)
+
+    new_pweight = 0.5 * (pweight + gossip(pweight))
+    new_numer = (0.5 * (stepped + gossip(stepped)))[None]
     return (new_numer, new_pweight)
 
 

time: 251 us -> 243 us (0.968)
  waiting for transfers between devices: 162 us -> 135 us
  starting transfers between devices: 33 us -> 50.2 us
  matrix products: 25.9 us -> 19 us
  other arithmetic: 7.58 us -> 13.7 us
  local copies, waits for them, and re-layouts: 4.1 us -> 6.82 us
    reduce_scatter x1, waiting for transfers between devices: 37.7 us -> 1.42 us  [on_device(): near = lax.psum_scatter(near, 'y', scatter_dimension=0, tiled=False)]
    ppermute x2, waiting for transfers between devices: 0.94 us -> 19.2 us  [from_partner(): lax.ppermute(shard, axis, [(i, i ^ 1 << apart) for i in range(lax.axis_si...]
    ppermute x2, starting transfers between devices: 18.5 us -> 35.8 us  [from_partner(): lax.ppermute(shard, axis, [(i, i ^ 1 << apart) for i in range(lax.axis_si...]
    ppermute x1, waiting for transfers between devices: 34.5 us -> 28.3 us  [on_device(): lax.ppermute(weight_rows, 'zh', swap_z)]
    add x0 -> x2, other arithmetic: none -> 5.23 us  [own_plus_other(): return own + sent]
    dot_general x4, matrix products: 13.8 us -> 9.13 us  [tm(): jnp.einsum('tyi,to->yio', a, dpre, preferred_element_type=jnp.float32)]
    ppermute x2, waiting for transfers between devices: 10.9 us -> 7.2 us  [own_plus_other(): sent = lax.ppermute(tm(a_other), 'core', swap_core)]
  transfers between devices with their start and end apart: 12 -> 12, of which waited for: 8 -> 10; matrix products, arithmetic and copies ran while one was open for 7% -> 9% of each run, Pallas kernels for 0% -> 0%
where the time goes in v4:
time: 243 us
  waiting for transfers between devices  135 us (56%)
  starting transfers between devices  50.2 us (21%)
  matrix products  19 us (8%)
  between operations  16.5 us (7%)
  other arithmetic  13.7 us (6%)
  local copies, waits for them, and re-layouts  6.82 us (3%)
    all_gather x1, waiting for transfers between devices, on_device(): w_far = lax.all_gather(w_cross, 'y', axis=0, tiled=False)  45 us
    ppermute x2, starting transfers between devices, from_partner(): lax.ppermute(shard, axis, [(i, i ^ 1 << apart) for i in range(lax.axis_si...  35.8 us
    reduce_scatter x1, waiting for transfers between devices, on_device(): lax.psum_scatter(far, 'y', scatter_dimension=0, tiled=False)  30.2 us
    ppermute x1, waiting for transfers between devices, on_device(): lax.ppermute(weight_rows, 'zh', swap_z)  28.3 us
    ppermute x2, waiting for transfers between devices, from_partner(): lax.ppermute(shard, axis, [(i, i ^ 1 << apart) for i in range(lax.axis_si...  19.2 us
    dot_general x4, matrix products, mm(): return jnp.einsum('tyi,yio->to', a, w, preferred_element_type=jnp.float32)  9.89 us
    dot_general x4, matrix products, tm(): jnp.einsum('tyi,to->yio', a, dpre, preferred_element_type=jnp.float32)  9.13 us
    ppermute x2, waiting for transfers between devices, own_plus_other(): sent = lax.ppermute(tm(a_other), 'core', swap_core)  7.2 us
  transfers between devices with their start and end apart: 12, of which 10 were waited for; matrix products, arithmetic and copies ran while one was open for 9% of the time, Pallas kernels for 0%

profile of v4, /device:TPU:2, one launch (start us, length us, event | category | flops | bytes accessed | tf_op | source)
XLA Modules:
  0.0 242.7 jit_solution(6815314763639916642)
XLA Ops:
  8.0 2.4 divide_convert_fusion
  11.5 7.2 %collective-permute-start.8 = (bf16[160,2560]{1,0:T(8,128)(2,1)}, bf16[160,2560]{1,0:T(8,128)(2,1)}, u32[]{:S(2)}, u32[]{:S(2)}) collective-permute-start(bf16[160,2560]{1,0:T(8,128)(2,1)} %fusion.12), channel_id=1, source_target_pairs={{0,8},{8,0},{1,9},{9,1},{2,10},{10,2},{3,11},{11,3},{4,12},{12,4},... | collective-permute-start | bytes 2457608 | tf_op jit(solution)/shard_map/ppermute | solution.py:45
  18.7 4.0 %copy.14 = bf16[1,384,2560]{1,2,0:T(8,128)(2,1)} copy(bf16[1,384,2560]{2,1,0:T(8,128)(2,1)} %param.15) | data formatting | bytes 3932160 | tf_op args[0]
  22.7 2.5 %dynamic-slice_bitcast_fusion = (bf16[384,4,160]{0,2,1:T(8,128)(2,1)}, bf16[384,4,160]{0,2,1:T(8,128)(2,1)S(1)}, bf16[384,4,160]{0,2,1:T(8,128)(2,1)S(1)}, bf16[384,4,160]{0,2,1:T(8,128)(2,1)S(1)}) fusion(bf16[384,2,4,2,160]{0,4,3,2,1:T(8,128)(2,1)} %bitcast.66, s32[]{:T(128)S(6)} %select_n.33, s32[]{:T(128)S(6)} %select_n.31, s32[]{:T(128)S(6)} %select_n.29, ...), kind=kLoop, calls=%fused_computation.27 | loop fusion | bytes 3932176 | tf_op jit(solution)/shard_map/jit(dynamic_index_in_dim)/squeeze | solution.py:39
  25.2 28.3 %collective-permute-done.8 = bf16[160,2560]{1,0:T(8,128)(2,1)} collective-permute-done((bf16[160,2560]{1,0:T(8,128)(2,1)}, bf16[160,2560]{1,0:T(8,128)(2,1)}, u32[]{:S(2)}, u32[]{:S(2)}) %collective-permute-start.8) | collective-permute-done | bytes 819232 | tf_op jit(solution)/shard_map/ppermute | solution.py:45
  53.5 3.2 %all-gather.4.cloned.1.call-done = bf16[4,160,2560]{2,1,0:T(8,128)(2,1)} async-done(((bf16[1,160,2560]{2,1,0:T(8,128)(2,1)}), bf16[4,160,2560]{2,1,0:T(8,128)(2,1)}) %all-gather.4.cloned.1.call-update) | async-done | bytes 3276816 | tf_op jit(solution)/shard_map/all_gather | solution.py:41
  56.9 45.0 %all-gather.6.cloned.1.call-done = bf16[640,2560]{1,0:T(8,128)(2,1)} async-done(((bf16[160,2560]{1,0:T(8,128)(2,1)}), bf16[640,2560]{1,0:T(8,128)(2,1)}) %all-gather.6.cloned.1.call-update) | async-done | bytes 3276816 | tf_op jit(solution)/shard_map/all_gather | solution.py:47
  101.9 3.8 %convolution_bitcast_fusion.2 = f32[384,2560]{1,0:T(8,128)S(1)} fusion(bf16[384,4,160]{0,2,1:T(8,128)(2,1)S(1)} %get-tuple-element.40, bf16[4,160,2560]{2,1,0:T(8,128)(2,1)} %collective-permute-done.9), kind=kOutput, calls=%fused_computation.6 | convolution fusion | flops 1258291200 | bytes 7700480 | tf_op jit(solution)/shard_map/tyi,yio->to/dot_general | solution.py:52
  105.7 1.7 convolution_bitcast_fusion.1
  110.0 2.6 %multiply_reduce_fusion = (f32[384]{0:T(512)S(1)}, f32[384,2560]{1,0:T(8,128)S(1)}) fusion(f32[384,2560]{1,0:T(8,128)S(1)} %convolution_bitcast_fusion, f32[384,2560]{1,0:T(8,128)S(1)} %convolution_bitcast_fusion.1, f32[384,2560]{1,0:T(8,128)S(1)} %convolution_bitcast_fusion.2, bf16[384,4,160]{0,2,1:T(8,128)(2,1)S(1)} %get-tuple-element.38, ...), kind=kOutput, calls=%fused_computation.18 | convolution fusion | flops 1265172096 | bytes 21464576 | tf_op jit(solution)/shard_map/tyi,yio->to/dot_general | solution.py:52
  114.5 1.9 convolution_convert_fusion
  117.1 1.9 convolution_convert_fusion.1
  119.0 3.6 %collective-permute-done.12 = bf16[4,160,2560]{2,1,0:T(8,128)(2,1)S(1)} collective-permute-done((bf16[4,160,2560]{2,1,0:T(8,128)(2,1)S(1)}, bf16[4,160,2560]{2,1,0:T(8,128)(2,1)S(1)}, u32[]{:S(2)}, u32[]{:S(2)}) %collective-permute-start.12) | collective-permute-done | bytes 3276832 | tf_op jit(solution)/shard_map/ppermute | solution.py:70
  122.6 2.6 %add.93 = bf16[4,160,2560]{2,1,0:T(8,128)(2,1)} add(bf16[4,160,2560]{2,1,0:T(8,128)(2,1)S(1)} %convolution_convert_fusion.1, bf16[4,160,2560]{2,1,0:T(8,128)(2,1)S(1)} %collective-permute-done.12) | non-fusion elementwise | flops 1638400 | bytes 9830400 | tf_op jit(solution)/shard_map/add | solution.py:72
  125.3 3.5 %convolution_convert_fusion.2 = bf16[4,160,2560]{2,1,0:T(8,128)(2,1)S(1)} fusion(bf16[384,4,160]{0,2,1:T(8,128)(2,1)S(1)} %get-tuple-element.40, bf16[384,2560,1]{1,0,2:T(8,128)(2,1)} %copy-done.4), kind=kOutput, calls=%fused_computation.2 | convolution fusion | flops 1259929600 | bytes 5734400 | tf_op jit(solution)/shard_map/tyi,to->yio/dot_general | solution.py:65
  129.3 1.9 convolution_convert_fusion.3
  131.2 3.6 %collective-permute-done.11 = bf16[4,160,2560]{2,1,0:T(8,128)(2,1)S(1)} collective-permute-done((bf16[4,160,2560]{2,1,0:T(8,128)(2,1)S(1)}, bf16[4,160,2560]{2,1,0:T(8,128)(2,1)S(1)}, u32[]{:S(2)}, u32[]{:S(2)}) %collective-permute-start.11) | collective-permute-done | bytes 3276832 | tf_op jit(solution)/shard_map/ppermute | solution.py:70
  134.8 2.6 %add.92 = bf16[4,160,2560]{2,1,0:T(8,128)(2,1)} add(bf16[4,160,2560]{2,1,0:T(8,128)(2,1)S(1)} %convolution_convert_fusion.3, bf16[4,160,2560]{2,1,0:T(8,128)(2,1)S(1)} %collective-permute-done.11) | non-fusion elementwise | flops 1638400 | bytes 9830400 | tf_op jit(solution)/shard_map/add | solution.py:72
  137.4 30.2 %reduce-scatter.5.cloned.1.call-done = bf16[1,160,2560]{2,1,0:T(8,128)(2,1)} async-done(((bf16[4,160,2560]{2,1,0:T(8,128)(2,1)}), bf16[1,160,2560]{2,1,0:T(8,128)(2,1)}) %reduce-scatter.5.cloned.1.call-update) | async-done | bytes 819216 | tf_op jit(solution)/shard_map/reduce_scatter | solution.py:75
  167.6 5.7 %collective-permute-start.13 = (bf16[160,2560]{1,0:T(8,128)(2,1)}, bf16[160,2560]{1,0:T(8,128)(2,1)}, u32[]{:S(2)}, u32[]{:S(2)}) collective-permute-start(bf16[160,2560]{1,0:T(8,128)(2,1)} %bitcast.69), channel_id=1, source_target_pairs={{0,8},{8,0},{1,9},{9,1},{2,10},{10,2},{3,11},{11,3},{4,12},{12,4},... | collective-permute-start | bytes 2457608 | tf_op jit(solution)/shard_map/ppermute | solution.py:75
  173.9 36.3 %conditional.9 = (f32[1]{0:T(128)}) conditional(s32[]{:T(128)} %bitcast.17, f32[1]{0:T(128)} %param.20, f32[1]{0:T(128)} %param.20, f32[1]{0:T(128)} %param.20, f32[1]{0:T(128)} %param.20), branch_computations={%region_8.9_spmd, %region_9.10_spmd, %region_10.11_spmd, %region_1... | conditional | flops 2 | bytes 68
  174.6 34.1 %collective-permute-start.6 = (bf16[1]{0:T(256)(128)(2,1)}, bf16[1]{0:T(256)(128)(2,1)}, u32[]{:S(2)}, u32[]{:S(2)}) collective-permute-start(bf16[1]{0:T(256)(128)(2,1)} %convert_element_type.92), channel_id=1, source_target_pairs={{0,64},{16,80},{32,96},{48,112},{64,0},{80,16},{96,32},{112,48},{1... | collective-permute-start | bytes 14 | tf_op jit(solution)/shard_map/cond/branch_2_fun/ppermute | solution.py:20
  213.4 20.3 %conditional.8 = (f32[160,2560]{1,0:T(8,128)S(1)}) conditional(s32[]{:T(128)} %bitcast.17, f32[160,2560]{1,0:T(8,128)S(1)} %fusion.11, f32[160,2560]{1,0:T(8,128)S(1)} %fusion.11, f32[160,2560]{1,0:T(8,128)S(1)} %fusion.11, f32[160,2560]{1,0:T(8,128)S(1)} %fusion.11), branch_computations={%region_4.5_spmd, %region_5.6_spmd, %region_6.7_spmd, %region_7.8_... | conditional | flops 819200 | bytes 8192048
  215.1 18.3 %collective-permute-done.2 = bf16[160,2560]{1,0:T(8,128)(2,1)S(1)} collective-permute-done((bf16[160,2560]{1,0:T(8,128)(2,1)S(1)}, bf16[160,2560]{1,0:T(8,128)(2,1)S(1)}, u32[]{:S(2)}, u32[]{:S(2)}) %collective-permute-start.2) | collective-permute-done | bytes 819232 | tf_op jit(solution)/shard_map/cond/branch_2_fun/ppermute | solution.py:20
  (46 shorter events, 14.0 us)
Async XLA Ops:
  7.2 3.3 %copy-start = (f32[1,160,2560]{2,1,0:T(8,128)S(1)}, f32[1,160,2560]{2,1,0:T(8,128)}, u32[]{:S(2)}) copy-start(f32[1,160,2560]{2,1,0:T(8,128)} %param.19) | copy-start | bytes 4915204
  7.2 49.5 %all-gather.4.cloned.1.call-start = ((), (), s32[]{:S(2)}) async-start(), calls=%async_computation.2 | async-start | bytes 4096000 | tf_op jit(solution)/shard_map/all_gather | solution.py:41
  10.4 91.5 %all-gather.6.cloned.1.call-start = ((), (), s32[]{:S(2)}) async-start(), calls=%async_computation.5 | async-start | bytes 4096000 | tf_op jit(solution)/shard_map/all_gather | solution.py:47
  11.5 42.0 %collective-permute-start.8 = (bf16[160,2560]{1,0:T(8,128)(2,1)}, bf16[160,2560]{1,0:T(8,128)(2,1)}, u32[]{:S(2)}, u32[]{:S(2)}) collective-permute-start(bf16[160,2560]{1,0:T(8,128)(2,1)} %fusion.12), channel_id=1, source_target_pairs={{0,8},{8,0},{1,9},{9,1},{2,10},{10,2},{3,11},{11,3},{4,12},{12,4},... | collective-permute-start | bytes 2457608 | tf_op jit(solution)/shard_map/ppermute | solution.py:45
  56.7 110.9 %reduce-scatter.5.cloned.1.call-start = ((), (), s32[]{:S(2)}) async-start(), calls=%async_computation.4 | async-start | bytes 4096000 | tf_op jit(solution)/shard_map/reduce_scatter | solution.py:75
  56.8 45.1 %collective-permute-start.9 = (bf16[4,160,2560]{2,1,0:T(8,128)(2,1)}, bf16[4,160,2560]{2,1,0:T(8,128)(2,1)}, u32[]{:S(2)}, u32[]{:S(2)}) collective-permute-start(bf16[4,160,2560]{2,1,0:T(8,128)(2,1)} %all-gather.4.cloned.1.call-done), channel_id=1, source_target_pairs={{0,1},{1,0},{2,3},{3,2},{4,5},{5,4},{6,7},{7,6},{8,9},{9,8},{10,11... | collective-permute-start | bytes 9830408 | tf_op jit(solution)/shard_map/ppermute | solution.py:48
  101.9 3.8 %copy-start.2 = (bf16[640,2560]{1,0:T(8,128)(2,1)S(1)}, bf16[640,2560]{1,0:T(8,128)(2,1)}, u32[]{:S(2)}) copy-start(bf16[640,2560]{1,0:T(8,128)(2,1)} %all-gather.6.cloned.1.call-done) | copy-start | bytes 9830404
  101.9 6.1 %collective-permute-start.10 = (bf16[4,160,2560]{2,1,0:T(8,128)(2,1)}, bf16[4,160,2560]{2,1,0:T(8,128)(2,1)S(1)}, u32[]{:S(2)}, u32[]{:S(2)}) collective-permute-start(bf16[4,160,2560]{2,1,0:T(8,128)(2,1)} %bitcast.67), channel_id=1, source_target_pairs={{0,1},{1,0},{2,3},{3,2},{4,5},{5,4},{6,7},{7,6},{8,9},{9,8},{10,11... | collective-permute-start | bytes 9830408 | tf_op jit(solution)/shard_map/ppermute | solution.py:49
  105.7 2.2 copy-start.7
  107.5 2.2 copy-start.3
  107.5 2.5 %copy-start.6 = (bf16[1,384,2560]{2,1,0:T(8,128)(2,1)S(1)}, bf16[1,384,2560]{2,1,0:T(8,128)(2,1)}, u32[]{:S(2)}) copy-start(bf16[1,384,2560]{2,1,0:T(8,128)(2,1)} %param.16) | copy-start | bytes 5898244
  110.0 2.6 %copy-start.1 = (bf16[1,384,2560]{2,1,0:T(8,128)(2,1)S(1)}, bf16[1,384,2560]{2,1,0:T(8,128)(2,1)}, u32[]{:S(2)}) copy-start(bf16[1,384,2560]{2,1,0:T(8,128)(2,1)} %param.17) | copy-start | bytes 5898244
  110.0 2.6 %copy-start.8 = (f32[2560]{0:T(1024)S(1)}, f32[2560]{0:T(1024)}, u32[]{:S(2)}) copy-start(f32[2560]{0:T(1024)} %param.18) | copy-start | bytes 30724
  114.5 2.6 %copy-start.4 = (bf16[384,2560,1]{1,0,2:T(8,128)(2,1)}, bf16[384,2560,1]{1,0,2:T(8,128)(2,1)S(1)}, u32[]{:S(2)}) copy-start(bf16[384,2560,1]{1,0,2:T(8,128)(2,1)S(1)} %fusion.9) | copy-start | bytes 5898244
  116.3 6.2 %collective-permute-start.12 = (bf16[4,160,2560]{2,1,0:T(8,128)(2,1)S(1)}, bf16[4,160,2560]{2,1,0:T(8,128)(2,1)S(1)}, u32[]{:S(2)}, u32[]{:S(2)}) collective-permute-start(bf16[4,160,2560]{2,1,0:T(8,128)(2,1)S(1)} %convolution_convert_fusion), channel_id=1, source_target_pairs={{0,1},{1,0},{2,3},{3,2},{4,5},{5,4},{6,7},{7,6},{8,9},{9,8},{10,11... | collective-permute-start | bytes 9830408 | tf_op jit(solution)/shard_map/ppermute | solution.py:70
  125.2 86.4 %reduce-scatter.3.cloned.1.call-start = ((), (), s32[]{:S(2)}) async-start(), calls=%async_computation.3 | async-start | bytes 4096000 | tf_op jit(solution)/shard_map/reduce_scatter | solution.py:77
  125.3 4.0 %copy-start.5 = (bf16[384,2560,1]{1,0,2:T(8,128)(2,1)S(1)}, bf16[384,2560,1]{1,0,2:T(8,128)(2,1)}, u32[]{:S(2)}) copy-start(bf16[384,2560,1]{1,0,2:T(8,128)(2,1)} %copy-done.4) | copy-start | bytes 5898244
  128.9 5.9 %collective-permute-start.11 = (bf16[4,160,2560]{2,1,0:T(8,128)(2,1)S(1)}, bf16[4,160,2560]{2,1,0:T(8,128)(2,1)S(1)}, u32[]{:S(2)}, u32[]{:S(2)}) collective-permute-start(bf16[4,160,2560]{2,1,0:T(8,128)(2,1)S(1)} %convolution_convert_fusion.2), channel_id=1, source_target_pairs={{0,1},{1,0},{2,3},{3,2},{4,5},{5,4},{6,7},{7,6},{8,9},{9,8},{10,11... | collective-permute-start | bytes 9830408 | tf_op jit(solution)/shard_map/ppermute | solution.py:70
  167.6 44.1 %collective-permute-start.13 = (bf16[160,2560]{1,0:T(8,128)(2,1)}, bf16[160,2560]{1,0:T(8,128)(2,1)}, u32[]{:S(2)}, u32[]{:S(2)}) collective-permute-start(bf16[160,2560]{1,0:T(8,128)(2,1)} %bitcast.69), channel_id=1, source_target_pairs={{0,8},{8,0},{1,9},{9,1},{2,10},{10,2},{3,11},{11,3},{4,12},{12,4},... | collective-permute-start | bytes 2457608 | tf_op jit(solution)/shard_map/ppermute | solution.py:75
  174.6 35.0 %collective-permute-start.6 = (bf16[1]{0:T(256)(128)(2,1)}, bf16[1]{0:T(256)(128)(2,1)}, u32[]{:S(2)}, u32[]{:S(2)}) collective-permute-start(bf16[1]{0:T(256)(128)(2,1)} %convert_element_type.92), channel_id=1, source_target_pairs={{0,64},{16,80},{32,96},{48,112},{64,0},{80,16},{96,32},{112,48},{1... | collective-permute-start | bytes 14 | tf_op jit(solution)/shard_map/cond/branch_2_fun/ppermute | solution.py:20
  213.5 20.0 %collective-permute-start.2 = (bf16[160,2560]{1,0:T(8,128)(2,1)S(1)}, bf16[160,2560]{1,0:T(8,128)(2,1)S(1)}, u32[]{:S(2)}, u32[]{:S(2)}) collective-permute-start(bf16[160,2560]{1,0:T(8,128)(2,1)S(1)} %convert_element_type.84), channel_id=1, source_target_pairs={{0,64},{16,80},{32,96},{48,112},{64,0},{80,16},{96,32},{112,48},{1... | collective-permute-start | bytes 2457608 | tf_op jit(solution)/shard_map/cond/branch_2_fun/ppermute | solution.py:20
Sparse Core Ops, SparseCore 0:
  10.5 46.0 all-gather.3
  58.5 43.3 all-gather.5
  125.4 42.1 reduce-scatter.4
  170.0 41.6 reduce-scatter.2

commit v5 on v4

--- a/solution.py
+++ b/solution.py
@@ -20,6 +20,36 @@
     return lax.ppermute(shard, axis, [(i, i ^ 1 << apart) for i in range(lax.axis_size(axis))])
 
 
+def ring_gather(piece, axis):
+    n = lax.axis_size(axis)
+    assert n == 4
+    cw = [(i, (i + 1) % n) for i in range(n)]
+    ccw = [(i, (i - 1) % n) for i in range(n)]
+    half = piece.shape[0] // 2
+    left = lax.ppermute(piece, axis, cw)
+    right = lax.ppermute(piece, axis, ccw)
+    opposite = jnp.concatenate(
+        [lax.ppermute(left[:half], axis, cw), lax.ppermute(right[half:], axis, ccw)], axis=0
+    )
+    return jnp.stack([piece, right, opposite, left])
+
+
+def ring_reduce(parts, axis):
+    n = lax.axis_size(axis)
+    assert n == 4
+    cw = [(i, (i + 1) % n) for i in range(n)]
+    ccw = [(i, (i - 1) % n) for i in range(n)]
+    half = parts.shape[1] // 2
+    f32 = parts.astype(jnp.float32)
+    got_a = lax.ppermute(parts[2, :half], axis, cw).astype(jnp.float32)
+    got_b = lax.ppermute(parts[2, half:], axis, ccw).astype(jnp.float32)
+    to_next = jnp.concatenate([f32[1, :half] + got_a, f32[1, half:]], axis=0)
+    to_prev = jnp.concatenate([f32[3, :half], f32[3, half:] + got_b], axis=0)
+    from_prev = lax.ppermute(to_next.astype(jnp.bfloat16), axis, cw).astype(jnp.float32)
+    from_next = lax.ppermute(to_prev.astype(jnp.bfloat16), axis, ccw).astype(jnp.float32)
+    return f32[0] + from_prev + from_next
+
+
 def on_device(attn, resid, cotangent, gain, numer, pweight, round_bit):
     n_zh = lax.axis_size("zh")
     n_y = lax.axis_size("y")
@@ -40,11 +70,13 @@
 
     w_near = lax.all_gather(weight_rows, "y", axis=0, tiled=False)
     a_nn, a_no = cols(me_z, me_c), cols(me_z, 1 - me_c)
-    a_fn, a_fo = cols(1 - me_z, me_c), cols(1 - me_z, 1 - me_c)
+    me_y = lax.axis_index("y")
+    a_fn = jnp.roll(cols(1 - me_z, me_c), -me_y, axis=1)
+    a_fo = jnp.roll(cols(1 - me_z, 1 - me_c), -me_y, axis=1)
     w_near, w_cross, a_nn, a_no, a_fn, a_fo = lax.optimization_barrier(
         (w_near, lax.ppermute(weight_rows, "zh", swap_z), a_nn, a_no, a_fn, a_fo)
     )
-    w_far = lax.all_gather(w_cross, "y", axis=0, tiled=False)
+    w_far = ring_gather(w_cross, "y")
     w_near_o = lax.ppermute(w_near, "core", swap_core)
     w_far_o = lax.ppermute(w_far, "core", swap_core)
 
@@ -72,7 +104,7 @@
         return own + sent
 
     far = own_plus_other(a_fn, a_fo)
-    far = lax.ppermute(lax.psum_scatter(far, "y", scatter_dimension=0, tiled=False), "zh", swap_z)
+    far = lax.ppermute(ring_reduce(far, "y").astype(jnp.bfloat16), "zh", swap_z)
     near = own_plus_other(a_nn, a_no)
     near = lax.psum_scatter(near, "y", scatter_dimension=0, tiled=False)
     grad = near.astype(jnp.float32) + far.astype(jnp.float32)

time: 243 us -> 262 us (1.078)
  the two profiles are of different devices: /device:TPU:2 before, /device:TPU:68 now
where the time goes in v5:
time: 262 us; the launch traced here: 266 us
  waiting for transfers between devices  175 us (67%)
  starting transfers between devices  27.8 us (11%)
  matrix products  19.8 us (8%)
  other arithmetic  16.9 us (6%)
  between operations  16.9 us (6%)
  local copies, waits for them, and re-layouts  7.78 us (3%)
    ppermute x2, waiting for transfers between devices, from_partner(): lax.ppermute(shard, axis, [(i, i ^ 1 << apart) for i in range(lax.axis_si...  66.5 us
    ppermute x1, waiting for transfers between devices, ring_reduce(): lax.ppermute(to_next.astype(jnp.bfloat16), axis, cw).astype(jnp.float32)  32.8 us
    ppermute x1, waiting for transfers between devices, on_device(): lax.ppermute(weight_rows, 'zh', swap_z)  29.6 us
    ppermute x1, waiting for transfers between devices, ring_gather(): left = lax.ppermute(piece, axis, cw)  18 us
    ppermute x1, waiting for transfers between devices, ring_reduce(): got_a = lax.ppermute(parts[2, :half], axis, cw).astype(jnp.float32)  14.6 us
    dot_general x4, matrix products, tm(): jnp.einsum('tyi,to->yio', a, dpre, preferred_element_type=jnp.float32)  10.7 us
    dot_general x4, matrix products, mm(): return jnp.einsum('tyi,yio->to', a, w, preferred_element_type=jnp.float32)  9.07 us
    ppermute x1, waiting for transfers between devices, ring_gather(): lax.ppermute(left[:half], axis, cw)  8.04 us
  transfers between devices with their start and end apart: 18, of which 10 were waited for; matrix products, arithmetic and copies ran while one was open for 11% of the time, Pallas kernels for 0%

profile of v5, /device:TPU:68, one launch (start us, length us, event | category | flops | bytes accessed | tf_op | source)
XLA Modules:
  0.0 265.7 jit_solution(6575774316697231297)
XLA Ops:
  11.5 5.4 %collective-permute-start.8 = (bf16[160,2560]{1,0:T(8,128)(2,1)}, bf16[160,2560]{1,0:T(8,128)(2,1)}, u32[]{:S(2)}, u32[]{:S(2)}) collective-permute-start(bf16[160,2560]{1,0:T(8,128)(2,1)} %fusion.15), channel_id=1, source_target_pairs={{0,8},{8,0},{1,9},{9,1},{2,10},{10,2},{3,11},{11,3},{4,12},{12,4},... | collective-permute-start | bytes 2457608 | tf_op jit(solution)/shard_map/ppermute | solution.py:77
  16.9 4.0 %copy.14 = bf16[1,384,2560]{1,2,0:T(8,128)(2,1)} copy(bf16[1,384,2560]{2,1,0:T(8,128)(2,1)} %param.17) | data formatting | bytes 3932160 | tf_op args[0]
  23.8 29.6 %collective-permute-done.8 = bf16[160,2560]{1,0:T(8,128)(2,1)} collective-permute-done((bf16[160,2560]{1,0:T(8,128)(2,1)}, bf16[160,2560]{1,0:T(8,128)(2,1)}, u32[]{:S(2)}, u32[]{:S(2)}) %collective-permute-start.8) | collective-permute-done | bytes 819232 | tf_op jit(solution)/shard_map/ppermute | solution.py:77
  53.4 2.5 all-gather.2.cloned.1.call-done
  56.6 2.5 collective-permute-start.10
  59.2 18.0 %collective-permute-done.11 = bf16[160,2560]{1,0:T(8,128)(2,1)S(1)} collective-permute-done((bf16[160,2560]{1,0:T(8,128)(2,1)}, bf16[160,2560]{1,0:T(8,128)(2,1)S(1)}, u32[]{:S(2)}, u32[]{:S(2)}) %collective-permute-start.11) | collective-permute-done | bytes 819232 | tf_op jit(solution)/shard_map/ppermute | solution.py:29
  77.4 3.3 %collective-permute-start.13 = (bf16[80,2560]{1,0:T(8,128)(2,1)S(1)}, bf16[80,2560]{1,0:T(8,128)(2,1)S(1)}, u32[]{:S(2)}, u32[]{:S(2)}) collective-permute-start(bf16[80,2560]{1,0:T(8,128)(2,1)S(1)} %slice.39), channel_id=1, source_target_pairs={{0,6},{2,0},{4,2},{6,4},{1,7},{3,1},{5,3},{7,5},{8,14},{10,8},{12,... | collective-permute-start | bytes 1228808 | tf_op jit(solution)/shard_map/ppermute | solution.py:32
  80.6 8.0 %collective-permute-done.12 = bf16[80,2560]{1,0:T(8,128)(2,1)S(1)} collective-permute-done((bf16[80,2560]{1,0:T(8,128)(2,1)S(1)}, bf16[80,2560]{1,0:T(8,128)(2,1)S(1)}, u32[]{:S(2)}, u32[]{:S(2)}) %collective-permute-start.12) | collective-permute-done | bytes 409632 | tf_op jit(solution)/shard_map/ppermute | solution.py:32
  90.6 3.0 %convolution_bitcast_fusion.1 = f32[384,2560]{1,0:T(8,128)S(1)} fusion(bf16[384,4,160]{0,2,1:T(8,128)(2,1)S(1)} %copy-done.6, bf16[1,160,2560]{2,1,0:T(8,128)(2,1)S(1)} %bitcast.98, bf16[1,160,2560]{2,1,0:T(8,128)(2,1)S(1)} %maximum_bitcast_fusion, bf16[1,160,2560]{2,1,0:T(8,128)(2,1)S(1)} %bitcast.100, bf16[1,160,2560]{2,1,0:T(8,128)(2,1)} %bitcast.10), kind=kOutput, calls=%fused_computation.5 | convolution fusion | flops 1263206400 | bytes 7700480 | tf_op jit(solution)/shard_map/tyi,yio->to/dot_general | solution.py:84
  98.2 2.6 multiply_reduce_fusion
  104.8 3.6 %convolution_convert_fusion = bf16[4,160,2560]{2,1,0:T(8,128)(2,1)} fusion(bf16[384,4,160]{0,2,1:T(8,128)(2,1)S(1)} %get-tuple-element.44, bf16[384,2560,1]{1,0,2:T(8,128)(2,1)S(1)} %fusion.9), kind=kOutput, calls=%fused_computation | convolution fusion | flops 1259929600 | bytes 5734400 | tf_op jit(solution)/shard_map/tyi,to->yio/dot_general | solution.py:97
  110.6 2.6 add.110
  114.2 3.4 %convolution_convert_fusion.1 = bf16[4,160,2560]{2,1,0:T(8,128)(2,1)S(1)} fusion(bf16[384,4,160]{0,2,1:T(8,128)(2,1)S(1)} %copy-done.7, bf16[384,2560,1]{1,0,2:T(8,128)(2,1)} %copy-done.3), kind=kOutput, calls=%fused_computation.1 | convolution fusion | flops 1259929600 | bytes 5734400 | tf_op jit(solution)/shard_map/tyi,to->yio/dot_general | solution.py:97
  117.6 2.6 fusion.22
  120.4 3.2 %collective-permute-start.19 = (bf16[80,2560]{1,0:T(8,128)(2,1)S(1)}, bf16[80,2560]{1,0:T(8,128)(2,1)S(1)}, u32[]{:S(2)}, u32[]{:S(2)}) collective-permute-start(bf16[80,2560]{1,0:T(8,128)(2,1)S(1)} %get-tuple-element.52), channel_id=1, source_target_pairs={{0,6},{2,0},{4,2},{6,4},{1,7},{3,1},{5,3},{7,5},{8,14},{10,8},{12,... | collective-permute-start | bytes 1228808 | tf_op jit(solution)/shard_map/ppermute | solution.py:45
  123.6 14.6 %collective-permute-done.17 = bf16[80,2560]{1,0:T(8,128)(2,1)S(1)} collective-permute-done((bf16[80,2560]{1,0:T(8,128)(2,1)S(1)}, bf16[80,2560]{1,0:T(8,128)(2,1)S(1)}, u32[]{:S(2)}, u32[]{:S(2)}) %collective-permute-start.17) | collective-permute-done | bytes 409632 | tf_op jit(solution)/shard_map/ppermute | solution.py:44
  140.7 3.7 %collective-permute-start.20 = (bf16[160,2560]{1,0:T(8,128)(2,1)S(1)}, bf16[160,2560]{1,0:T(8,128)(2,1)S(1)}, u32[]{:S(2)}, u32[]{:S(2)}) collective-permute-start(bf16[160,2560]{1,0:T(8,128)(2,1)S(1)} %pad_maximum_fusion.2), channel_id=1, source_target_pairs={{0,6},{2,0},{4,2},{6,4},{1,7},{3,1},{5,3},{7,5},{8,14},{10,8},{12,... | collective-permute-start | bytes 2457608 | tf_op jit(solution)/shard_map/ppermute | solution.py:49
  144.4 32.8 %collective-permute-done.18 = bf16[160,2560]{1,0:T(8,128)(2,1)S(1)} collective-permute-done((bf16[160,2560]{1,0:T(8,128)(2,1)S(1)}, bf16[160,2560]{1,0:T(8,128)(2,1)S(1)}, u32[]{:S(2)}, u32[]{:S(2)}) %collective-permute-start.18) | collective-permute-done | bytes 819232 | tf_op jit(solution)/shard_map/ppermute | solution.py:48
  177.4 4.0 %collective-permute-start.21 = (bf16[160,2560]{1,0:T(8,128)(2,1)S(1)}, bf16[160,2560]{1,0:T(8,128)(2,1)S(1)}, u32[]{:S(2)}, u32[]{:S(2)}) collective-permute-start(bf16[160,2560]{1,0:T(8,128)(2,1)S(1)} %fusion.12), channel_id=1, source_target_pairs={{0,8},{8,0},{1,9},{9,1},{2,10},{10,2},{3,11},{11,3},{4,12},{12,4},... | collective-permute-start | bytes 2457608 | tf_op jit(solution)/shard_map/ppermute | solution.py:107
  182.1 37.1 %conditional.9 = (f32[1]{0:T(128)}) conditional(s32[]{:T(128)} %bitcast.26, f32[1]{0:T(128)} %param.22, f32[1]{0:T(128)} %param.22, f32[1]{0:T(128)} %param.22, f32[1]{0:T(128)} %param.22), branch_computations={%region_7.9_spmd, %region_8.10_spmd, %region_9.11_spmd, %region_10... | conditional | flops 2 | bytes 68
  182.8 3.6 %collective-permute-start.7 = (bf16[1]{0:T(256)(128)(2,1)}, bf16[1]{0:T(256)(128)(2,1)}, u32[]{:S(2)}, u32[]{:S(2)}) collective-permute-start(bf16[1]{0:T(256)(128)(2,1)} %convert_element_type.108), channel_id=1, source_target_pairs={{0,128},{16,144},{32,160},{48,176},{64,192},{80,208},{96,224},{112... | collective-permute-start | bytes 14 | tf_op jit(solution)/shard_map/cond/branch_3_fun/ppermute | solution.py:20
  186.3 32.2 %collective-permute-done.7 = bf16[1]{0:T(256)(128)(2,1)} collective-permute-done((bf16[1]{0:T(256)(128)(2,1)}, bf16[1]{0:T(256)(128)(2,1)}, u32[]{:S(2)}, u32[]{:S(2)}) %collective-permute-start.7) | collective-permute-done | bytes 34 | tf_op jit(solution)/shard_map/cond/branch_3_fun/ppermute | solution.py:20
  221.8 34.6 %conditional.8 = (f32[160,2560]{1,0:T(8,128)S(1)}) conditional(s32[]{:T(128)} %bitcast.26, f32[160,2560]{1,0:T(8,128)S(1)} %fusion.14, f32[160,2560]{1,0:T(8,128)S(1)} %fusion.14, f32[160,2560]{1,0:T(8,128)S(1)} %fusion.14, f32[160,2560]{1,0:T(8,128)S(1)} %fusion.14), branch_computations={%region_3.5_spmd, %region_4.6_spmd, %region_5.7_spmd, %region_6.8_... | conditional | flops 819200 | bytes 8192048
  222.0 34.3 %collective-permute-done.3 = bf16[160,2560]{1,0:T(8,128)(2,1)S(1)} collective-permute-done((bf16[160,2560]{1,0:T(8,128)(2,1)S(1)}, bf16[160,2560]{1,0:T(8,128)(2,1)S(1)}, u32[]{:S(2)}, u32[]{:S(2)}) %collective-permute-start.3) | collective-permute-done | bytes 819232 | tf_op jit(solution)/shard_map/cond/branch_3_fun/ppermute | solution.py:20
  (66 shorter events, 28.0 us)
Async XLA Ops:
  7.2 3.3 %copy-start = (f32[1,160,2560]{2,1,0:T(8,128)S(1)}, f32[1,160,2560]{2,1,0:T(8,128)}, u32[]{:S(2)}) copy-start(f32[1,160,2560]{2,1,0:T(8,128)} %param.21) | copy-start | bytes 4915204
  7.2 48.8 %all-gather.2.cloned.1.call-start = ((), (), s32[]{:S(2)}) async-start(), calls=%async_computation.1 | async-start | bytes 4096000 | tf_op jit(solution)/shard_map/all_gather | solution.py:71
  10.4 209.6 %reduce-scatter.2.cloned.1.call-start = ((), (), s32[]{:S(2)}) async-start(), calls=%async_computation.2 | async-start | bytes 4096000 | tf_op jit(solution)/shard_map/reduce_scatter | solution.py:109
  11.5 41.9 %collective-permute-start.8 = (bf16[160,2560]{1,0:T(8,128)(2,1)}, bf16[160,2560]{1,0:T(8,128)(2,1)}, u32[]{:S(2)}, u32[]{:S(2)}) collective-permute-start(bf16[160,2560]{1,0:T(8,128)(2,1)} %fusion.15), channel_id=1, source_target_pairs={{0,8},{8,0},{1,9},{9,1},{2,10},{10,2},{3,11},{11,3},{4,12},{12,4},... | collective-permute-start | bytes 2457608 | tf_op jit(solution)/shard_map/ppermute | solution.py:77
  55.9 21.2 %collective-permute-start.11 = (bf16[160,2560]{1,0:T(8,128)(2,1)}, bf16[160,2560]{1,0:T(8,128)(2,1)S(1)}, u32[]{:S(2)}, u32[]{:S(2)}) collective-permute-start(bf16[160,2560]{1,0:T(8,128)(2,1)} %collective-permute-done.8), channel_id=1, source_target_pairs={{0,2},{2,4},{4,6},{6,0},{1,3},{3,5},{5,7},{7,1},{8,10},{10,12},{12... | collective-permute-start | bytes 2457608 | tf_op jit(solution)/shard_map/ppermute | solution.py:29
  56.6 20.7 %collective-permute-start.10 = (bf16[160,2560]{1,0:T(8,128)(2,1)}, bf16[160,2560]{1,0:T(8,128)(2,1)S(1)}, u32[]{:S(2)}, u32[]{:S(2)}) collective-permute-start(bf16[160,2560]{1,0:T(8,128)(2,1)} %collective-permute-done.8), channel_id=1, source_target_pairs={{0,6},{2,0},{4,2},{6,4},{1,7},{3,1},{5,3},{7,5},{8,14},{10,8},{12,... | collective-permute-start | bytes 2457608 | tf_op jit(solution)/shard_map/ppermute | solution.py:30
  77.2 11.5 %collective-permute-start.12 = (bf16[80,2560]{1,0:T(8,128)(2,1)S(1)}, bf16[80,2560]{1,0:T(8,128)(2,1)S(1)}, u32[]{:S(2)}, u32[]{:S(2)}) collective-permute-start(bf16[80,2560]{1,0:T(8,128)(2,1)S(1)} %slice.38), channel_id=1, source_target_pairs={{0,2},{2,4},{4,6},{6,0},{1,3},{3,5},{5,7},{7,1},{8,10},{10,12},{12... | collective-permute-start | bytes 1228808 | tf_op jit(solution)/shard_map/ppermute | solution.py:32
  77.4 11.3 %collective-permute-start.13 = (bf16[80,2560]{1,0:T(8,128)(2,1)S(1)}, bf16[80,2560]{1,0:T(8,128)(2,1)S(1)}, u32[]{:S(2)}, u32[]{:S(2)}) collective-permute-start(bf16[80,2560]{1,0:T(8,128)(2,1)S(1)} %slice.39), channel_id=1, source_target_pairs={{0,6},{2,0},{4,2},{6,4},{1,7},{3,1},{5,3},{7,5},{8,14},{10,8},{12,... | collective-permute-start | bytes 1228808 | tf_op jit(solution)/shard_map/ppermute | solution.py:32
  80.6 13.0 %collective-permute-start.9 = (bf16[4,160,2560]{2,1,0:T(8,128)(2,1)}, bf16[4,160,2560]{2,1,0:T(8,128)(2,1)S(1)}, u32[]{:S(2)}, u32[]{:S(2)}) collective-permute-start(bf16[4,160,2560]{2,1,0:T(8,128)(2,1)} %all-gather.2.cloned.1.call-done), channel_id=1, source_target_pairs={{0,1},{1,0},{2,3},{3,2},{4,5},{5,4},{6,7},{7,6},{8,9},{9,8},{10,11... | collective-permute-start | bytes 9830408 | tf_op jit(solution)/shard_map/ppermute | solution.py:80
  90.3 6.1 %collective-permute-start.14 = (bf16[4,160,2560]{2,1,0:T(8,128)(2,1)S(1)}, bf16[4,160,2560]{2,1,0:T(8,128)(2,1)S(1)}, u32[]{:S(2)}, u32[]{:S(2)}) collective-permute-start(bf16[4,160,2560]{2,1,0:T(8,128)(2,1)S(1)} %pad_maximum_fusion), channel_id=1, source_target_pairs={{0,1},{1,0},{2,3},{3,2},{4,5},{5,4},{6,7},{7,6},{8,9},{9,8},{10,11... | collective-permute-start | bytes 9830408 | tf_op jit(solution)/shard_map/ppermute | solution.py:81
  95.3 2.8 %copy-start.2 = (bf16[4,160,2560]{2,1,0:T(8,128)(2,1)S(1)}, bf16[4,160,2560]{2,1,0:T(8,128)(2,1)}, u32[]{:S(2)}) copy-start(bf16[4,160,2560]{2,1,0:T(8,128)(2,1)} %all-gather.2.cloned.1.call-done) | copy-start | bytes 9830404
  95.3 2.8 %copy-start.4 = (bf16[1,384,2560]{2,1,0:T(8,128)(2,1)S(1)}, bf16[1,384,2560]{2,1,0:T(8,128)(2,1)}, u32[]{:S(2)}) copy-start(bf16[1,384,2560]{2,1,0:T(8,128)(2,1)} %param.18) | copy-start | bytes 5898244
  98.1 2.7 copy-start.1
  98.1 2.7 copy-start.8
  102.6 6.1 %copy-start.3 = (bf16[384,2560,1]{1,0,2:T(8,128)(2,1)}, bf16[384,2560,1]{1,0,2:T(8,128)(2,1)S(1)}, u32[]{:S(2)}) copy-start(bf16[384,2560,1]{1,0,2:T(8,128)(2,1)S(1)} %fusion.9) | copy-start | bytes 5898244
  104.5 6.1 %collective-permute-start.15 = (bf16[4,160,2560]{2,1,0:T(8,128)(2,1)S(1)}, bf16[4,160,2560]{2,1,0:T(8,128)(2,1)S(1)}, u32[]{:S(2)}, u32[]{:S(2)}) collective-permute-start(bf16[4,160,2560]{2,1,0:T(8,128)(2,1)S(1)} %convolution_convert_fusion.2), channel_id=1, source_target_pairs={{0,1},{1,0},{2,3},{3,2},{4,5},{5,4},{6,7},{7,6},{8,9},{9,8},{10,11... | collective-permute-start | bytes 9830408 | tf_op jit(solution)/shard_map/ppermute | solution.py:102
  108.4 9.2 %collective-permute-start.16 = (bf16[4,160,2560]{2,1,0:T(8,128)(2,1)}, bf16[4,160,2560]{2,1,0:T(8,128)(2,1)}, u32[]{:S(2)}, u32[]{:S(2)}) collective-permute-start(bf16[4,160,2560]{2,1,0:T(8,128)(2,1)} %convolution_convert_fusion), channel_id=1, source_target_pairs={{0,1},{1,0},{2,3},{3,2},{4,5},{5,4},{6,7},{7,6},{8,9},{9,8},{10,11... | collective-permute-start | bytes 9830408 | tf_op jit(solution)/shard_map/ppermute | solution.py:102
  120.3 17.9 %collective-permute-start.17 = (bf16[80,2560]{1,0:T(8,128)(2,1)S(1)}, bf16[80,2560]{1,0:T(8,128)(2,1)S(1)}, u32[]{:S(2)}, u32[]{:S(2)}) collective-permute-start(bf16[80,2560]{1,0:T(8,128)(2,1)S(1)} %get-tuple-element.49), channel_id=1, source_target_pairs={{0,2},{2,4},{4,6},{6,0},{1,3},{3,5},{5,7},{7,1},{8,10},{10,12},{12... | collective-permute-start | bytes 1228808 | tf_op jit(solution)/shard_map/ppermute | solution.py:44
  120.4 19.9 %collective-permute-start.19 = (bf16[80,2560]{1,0:T(8,128)(2,1)S(1)}, bf16[80,2560]{1,0:T(8,128)(2,1)S(1)}, u32[]{:S(2)}, u32[]{:S(2)}) collective-permute-start(bf16[80,2560]{1,0:T(8,128)(2,1)S(1)} %get-tuple-element.52), channel_id=1, source_target_pairs={{0,6},{2,0},{4,2},{6,4},{1,7},{3,1},{5,3},{7,5},{8,14},{10,8},{12,... | collective-permute-start | bytes 1228808 | tf_op jit(solution)/shard_map/ppermute | solution.py:45
  140.5 36.7 %collective-permute-start.18 = (bf16[160,2560]{1,0:T(8,128)(2,1)S(1)}, bf16[160,2560]{1,0:T(8,128)(2,1)S(1)}, u32[]{:S(2)}, u32[]{:S(2)}) collective-permute-start(bf16[160,2560]{1,0:T(8,128)(2,1)S(1)} %pad_maximum_fusion.1), channel_id=1, source_target_pairs={{0,2},{2,4},{4,6},{6,0},{1,3},{3,5},{5,7},{7,1},{8,10},{10,12},{12... | collective-permute-start | bytes 2457608 | tf_op jit(solution)/shard_map/ppermute | solution.py:48
  140.7 36.5 %collective-permute-start.20 = (bf16[160,2560]{1,0:T(8,128)(2,1)S(1)}, bf16[160,2560]{1,0:T(8,128)(2,1)S(1)}, u32[]{:S(2)}, u32[]{:S(2)}) collective-permute-start(bf16[160,2560]{1,0:T(8,128)(2,1)S(1)} %pad_maximum_fusion.2), channel_id=1, source_target_pairs={{0,6},{2,0},{4,2},{6,4},{1,7},{3,1},{5,3},{7,5},{8,14},{10,8},{12,... | collective-permute-start | bytes 2457608 | tf_op jit(solution)/shard_map/ppermute | solution.py:49
  177.4 41.8 %collective-permute-start.21 = (bf16[160,2560]{1,0:T(8,128)(2,1)S(1)}, bf16[160,2560]{1,0:T(8,128)(2,1)S(1)}, u32[]{:S(2)}, u32[]{:S(2)}) collective-permute-start(bf16[160,2560]{1,0:T(8,128)(2,1)S(1)} %fusion.12), channel_id=1, source_target_pairs={{0,8},{8,0},{1,9},{9,1},{2,10},{10,2},{3,11},{11,3},{4,12},{12,4},... | collective-permute-start | bytes 2457608 | tf_op jit(solution)/shard_map/ppermute | solution.py:107
  182.8 35.8 %collective-permute-start.7 = (bf16[1]{0:T(256)(128)(2,1)}, bf16[1]{0:T(256)(128)(2,1)}, u32[]{:S(2)}, u32[]{:S(2)}) collective-permute-start(bf16[1]{0:T(256)(128)(2,1)} %convert_element_type.108), channel_id=1, source_target_pairs={{0,128},{16,144},{32,160},{48,176},{64,192},{80,208},{96,224},{112... | collective-permute-start | bytes 14 | tf_op jit(solution)/shard_map/cond/branch_3_fun/ppermute | solution.py:20
  221.9 34.4 %collective-permute-start.3 = (bf16[160,2560]{1,0:T(8,128)(2,1)S(1)}, bf16[160,2560]{1,0:T(8,128)(2,1)S(1)}, u32[]{:S(2)}, u32[]{:S(2)}) collective-permute-start(bf16[160,2560]{1,0:T(8,128)(2,1)S(1)} %convert_element_type.100), channel_id=1, source_target_pairs={{0,128},{16,144},{32,160},{48,176},{64,192},{80,208},{96,224},{112... | collective-permute-start | bytes 2457608 | tf_op jit(solution)/shard_map/cond/branch_3_fun/ppermute | solution.py:20
  (3 other events, 3.7 us)
Sparse Core Ops, SparseCore 0:
  10.6 45.3 all-gather.1
  113.3 63.3 reduce-scatter.1

commit v6 on v5

--- a/solution.py
+++ b/solution.py
@@ -104,8 +104,10 @@
         return own + sent
 
     far = own_plus_other(a_fn, a_fo)
-    far = lax.ppermute(ring_reduce(far, "y").astype(jnp.bfloat16), "zh", swap_z)
+    far = ring_reduce(far, "y").astype(jnp.bfloat16)
     near = own_plus_other(a_nn, a_no)
+    near, far = lax.optimization_barrier((near, far))
+    far = lax.ppermute(far, "zh", swap_z)
     near = lax.psum_scatter(near, "y", scatter_dimension=0, tiled=False)
     grad = near.astype(jnp.float32) + far.astype(jnp.float32)
     stepped = numer[0] - learning_rate * grad

time: 262 us -> 226 us (0.86)
  the two profiles are of different devices: /device:TPU:68 before, /device:TPU:2 now
where the time goes in v6:
time: 226 us; the launch traced here: 225 us
  waiting for transfers between devices  136 us (60%)
  starting transfers between devices  27.3 us (12%)
  matrix products  18.3 us (8%)
  other arithmetic  17.9 us (8%)
  between operations  16.9 us (7%)
  local copies, waits for them, and re-layouts  6.8 us (3%)
    ppermute x1, waiting for transfers between devices, on_device(): far = lax.ppermute(far, 'zh', swap_z)  27.9 us
    ppermute x1, waiting for transfers between devices, on_device(): lax.ppermute(weight_rows, 'zh', swap_z)  27.9 us
    ppermute x2, waiting for transfers between devices, from_partner(): lax.ppermute(shard, axis, [(i, i ^ 1 << apart) for i in range(lax.axis_si...  21 us
    ppermute x1, waiting for transfers between devices, ring_gather(): right = lax.ppermute(piece, axis, ccw)  18 us
    ppermute x1, waiting for transfers between devices, ring_reduce(): lax.ppermute(to_prev.astype(jnp.bfloat16), axis, ccw).astype(jnp.float32)  11.2 us
    ppermute x1, waiting for transfers between devices, ring_reduce(): got_a = lax.ppermute(parts[2, :half], axis, cw).astype(jnp.float32)  9.52 us
    dot_general x4, matrix products, tm(): jnp.einsum('tyi,to->yio', a, dpre, preferred_element_type=jnp.float32)  9.21 us
    dot_general x4, matrix products, mm(): return jnp.einsum('tyi,yio->to', a, w, preferred_element_type=jnp.float32)  9.07 us
  transfers between devices with their start and end apart: 18, of which 13 were waited for; matrix products, arithmetic and copies ran while one was open for 12% of the time, Pallas kernels for 0%

profile of v6, /device:TPU:2, one launch (start us, length us, event | category | flops | bytes accessed | tf_op | source)
XLA Modules:
  0.0 224.8 jit_solution(17295749043897228467)
XLA Ops:
  8.0 2.4 %divide_convert_fusion = bf16[1,160,2560]{2,1,0:T(8,128)(2,1)} fusion(f32[1,160,2560]{2,1,0:T(8,128)} %param.21, f32[]{:T(128)} %bitcast.94), kind=kLoop, calls=%fused_computation.31 | loop fusion | flops 819200 | bytes 2457604 | tf_op jit(solution)/shard_map/convert_element_type | solution.py:60
  11.5 7.2 %collective-permute-start.8 = (bf16[160,2560]{1,0:T(8,128)(2,1)}, bf16[160,2560]{1,0:T(8,128)(2,1)}, u32[]{:S(2)}, u32[]{:S(2)}) collective-permute-start(bf16[160,2560]{1,0:T(8,128)(2,1)} %fusion.15), channel_id=1, source_target_pairs={{0,8},{8,0},{1,9},{9,1},{2,10},{10,2},{3,11},{11,3},{4,12},{12,4},... | collective-permute-start | bytes 2457608 | tf_op jit(solution)/shard_map/ppermute | solution.py:77
  18.7 4.0 %copy.14 = bf16[1,384,2560]{1,2,0:T(8,128)(2,1)} copy(bf16[1,384,2560]{2,1,0:T(8,128)(2,1)} %param.17) | data formatting | bytes 3932160 | tf_op args[0]
  25.6 27.9 %collective-permute-done.8 = bf16[160,2560]{1,0:T(8,128)(2,1)} collective-permute-done((bf16[160,2560]{1,0:T(8,128)(2,1)}, bf16[160,2560]{1,0:T(8,128)(2,1)}, u32[]{:S(2)}, u32[]{:S(2)}) %collective-permute-start.8) | collective-permute-done | bytes 819232 | tf_op jit(solution)/shard_map/ppermute | solution.py:77
  53.5 3.2 %all-gather.2.cloned.1.call-done = bf16[4,160,2560]{2,1,0:T(8,128)(2,1)} async-done(((bf16[1,160,2560]{2,1,0:T(8,128)(2,1)}), bf16[4,160,2560]{2,1,0:T(8,128)(2,1)}) %all-gather.2.cloned.1.call-update) | async-done | bytes 3276816 | tf_op jit(solution)/shard_map/all_gather | solution.py:71
  58.7 18.0 %collective-permute-done.10 = bf16[160,2560]{1,0:T(8,128)(2,1)S(1)} collective-permute-done((bf16[160,2560]{1,0:T(8,128)(2,1)}, bf16[160,2560]{1,0:T(8,128)(2,1)S(1)}, u32[]{:S(2)}, u32[]{:S(2)}) %collective-permute-start.10) | collective-permute-done | bytes 819232 | tf_op jit(solution)/shard_map/ppermute | solution.py:30
  76.8 2.3 %collective-permute-start.13 = (bf16[80,2560]{1,0:T(8,128)(2,1)S(1)}, bf16[80,2560]{1,0:T(8,128)(2,1)S(1)}, u32[]{:S(2)}, u32[]{:S(2)}) collective-permute-start(bf16[80,2560]{1,0:T(8,128)(2,1)S(1)} %slice.39), channel_id=1, source_target_pairs={{0,6},{2,0},{4,2},{6,4},{1,7},{3,1},{5,3},{7,5},{8,14},{10,8},{12,... | collective-permute-start | bytes 1228808 | tf_op jit(solution)/shard_map/ppermute | solution.py:32
  79.2 7.8 %collective-permute-done.13 = bf16[80,2560]{1,0:T(8,128)(2,1)S(1)} collective-permute-done((bf16[80,2560]{1,0:T(8,128)(2,1)S(1)}, bf16[80,2560]{1,0:T(8,128)(2,1)S(1)}, u32[]{:S(2)}, u32[]{:S(2)}) %collective-permute-start.13) | collective-permute-done | bytes 409632 | tf_op jit(solution)/shard_map/ppermute | solution.py:32
  87.0 3.2 %collective-permute-done.12 = bf16[80,2560]{1,0:T(8,128)(2,1)S(1)} collective-permute-done((bf16[80,2560]{1,0:T(8,128)(2,1)S(1)}, bf16[80,2560]{1,0:T(8,128)(2,1)S(1)}, u32[]{:S(2)}, u32[]{:S(2)}) %collective-permute-start.12) | collective-permute-done | bytes 409632 | tf_op jit(solution)/shard_map/ppermute | solution.py:32
  92.1 3.0 %convolution_bitcast_fusion.1 = f32[384,2560]{1,0:T(8,128)S(1)} fusion(bf16[384,4,160]{0,2,1:T(8,128)(2,1)S(1)} %copy-done.8, bf16[1,160,2560]{2,1,0:T(8,128)(2,1)S(1)} %bitcast.100, bf16[1,160,2560]{2,1,0:T(8,128)(2,1)S(1)} %maximum_bitcast_fusion, bf16[1,160,2560]{2,1,0:T(8,128)(2,1)S(1)} %bitcast.98, bf16[1,160,2560]{2,1,0:T(8,128)(2,1)} %bitcast.10), kind=kOutput, calls=%fused_computation.5 | convolution fusion | flops 1263206400 | bytes 7700480 | tf_op jit(solution)/shard_map/tyi,yio->to/dot_general | solution.py:84
  99.7 2.6 %multiply_reduce_fusion = (f32[384]{0:T(512)S(1)}, f32[384,2560]{1,0:T(8,128)S(1)}) fusion(f32[384,2560]{1,0:T(8,128)S(1)} %convolution_bitcast_fusion, f32[384,2560]{1,0:T(8,128)S(1)} %convolution_bitcast_fusion.1, f32[384,2560]{1,0:T(8,128)S(1)} %convolution_bitcast_fusion.2, bf16[384,4,160]{0,2,1:T(8,128)(2,1)S(1)} %get-tuple-element.41, ...), kind=kOutput, calls=%fused_computation.18 | convolution fusion | flops 1265172096 | bytes 21464576 | tf_op jit(solution)/shard_map/tyi,yio->to/dot_general | solution.py:84
  106.4 3.6 %convolution_convert_fusion.2 = bf16[4,160,2560]{2,1,0:T(8,128)(2,1)} fusion(bf16[384,4,160]{0,2,1:T(8,128)(2,1)S(1)} %get-tuple-element.43, bf16[384,2560,1]{1,0,2:T(8,128)(2,1)S(1)} %fusion.9), kind=kOutput, calls=%fused_computation.2 | convolution fusion | flops 1259929600 | bytes 5734400 | tf_op jit(solution)/shard_map/tyi,to->yio/dot_general | solution.py:97
  113.1 3.2 %collective-permute-start.19 = (bf16[80,2560]{1,0:T(8,128)(2,1)S(1)}, bf16[80,2560]{1,0:T(8,128)(2,1)S(1)}, u32[]{:S(2)}, u32[]{:S(2)}) collective-permute-start(bf16[80,2560]{1,0:T(8,128)(2,1)S(1)} %get-tuple-element.56), channel_id=1, source_target_pairs={{0,6},{2,0},{4,2},{6,4},{1,7},{3,1},{5,3},{7,5},{8,14},{10,8},{12,... | collective-permute-start | bytes 1228808 | tf_op jit(solution)/shard_map/ppermute | solution.py:45
  116.3 9.5 %collective-permute-done.17 = bf16[80,2560]{1,0:T(8,128)(2,1)S(1)} collective-permute-done((bf16[80,2560]{1,0:T(8,128)(2,1)S(1)}, bf16[80,2560]{1,0:T(8,128)(2,1)S(1)}, u32[]{:S(2)}, u32[]{:S(2)}) %collective-permute-start.17) | collective-permute-done | bytes 409632 | tf_op jit(solution)/shard_map/ppermute | solution.py:44
  126.1 3.0 %collective-permute-start.20 = (bf16[160,2560]{1,0:T(8,128)(2,1)S(1)}, bf16[160,2560]{1,0:T(8,128)(2,1)}, u32[]{:S(2)}, u32[]{:S(2)}) collective-permute-start(bf16[160,2560]{1,0:T(8,128)(2,1)S(1)} %pad_maximum_fusion.2), channel_id=1, source_target_pairs={{0,6},{2,0},{4,2},{6,4},{1,7},{3,1},{5,3},{7,5},{8,14},{10,8},{12,... | collective-permute-start | bytes 2457608 | tf_op jit(solution)/shard_map/ppermute | solution.py:49
  131.9 2.7 %add.110 = bf16[4,160,2560]{2,1,0:T(8,128)(2,1)} add(bf16[4,160,2560]{2,1,0:T(8,128)(2,1)S(1)} %convolution_convert_fusion.3, bf16[4,160,2560]{2,1,0:T(8,128)(2,1)S(1)} %collective-permute-done.15) | non-fusion elementwise | flops 1638400 | bytes 9830400 | tf_op jit(solution)/shard_map/add | solution.py:104
  134.6 11.2 %collective-permute-done.20 = bf16[160,2560]{1,0:T(8,128)(2,1)} collective-permute-done((bf16[160,2560]{1,0:T(8,128)(2,1)S(1)}, bf16[160,2560]{1,0:T(8,128)(2,1)}, u32[]{:S(2)}, u32[]{:S(2)}) %collective-permute-start.20) | collective-permute-done | bytes 819232 | tf_op jit(solution)/shard_map/ppermute | solution.py:49
  145.8 4.7 %collective-permute-done.18 = bf16[160,2560]{1,0:T(8,128)(2,1)} collective-permute-done((bf16[160,2560]{1,0:T(8,128)(2,1)}, bf16[160,2560]{1,0:T(8,128)(2,1)}, u32[]{:S(2)}, u32[]{:S(2)}) %collective-permute-start.18) | collective-permute-done | bytes 819232 | tf_op jit(solution)/shard_map/ppermute | solution.py:48
  150.5 2.2 fusion.12
  152.7 5.8 %collective-permute-start.21 = (bf16[160,2560]{1,0:T(8,128)(2,1)S(1)}, bf16[160,2560]{1,0:T(8,128)(2,1)S(1)}, u32[]{:S(2)}, u32[]{:S(2)}) collective-permute-start(bf16[160,2560]{1,0:T(8,128)(2,1)S(1)} %fusion.12), channel_id=1, source_target_pairs={{0,8},{8,0},{1,9},{9,1},{2,10},{10,2},{3,11},{11,3},{4,12},{12,4},... | collective-permute-start | bytes 2457608 | tf_op jit(solution)/shard_map/ppermute | solution.py:110
  159.1 4.9 %conditional.9 = (f32[1]{0:T(128)}) conditional(s32[]{:T(128)} %bitcast.26, f32[1]{0:T(128)} %param.22, f32[1]{0:T(128)} %param.22, f32[1]{0:T(128)} %param.22, f32[1]{0:T(128)} %param.22), branch_computations={%region_7.9_spmd, %region_8.10_spmd, %region_9.11_spmd, %region_10... | conditional | flops 2 | bytes 68
  164.0 27.9 %collective-permute-done.21 = bf16[160,2560]{1,0:T(8,128)(2,1)S(1)} collective-permute-done((bf16[160,2560]{1,0:T(8,128)(2,1)S(1)}, bf16[160,2560]{1,0:T(8,128)(2,1)S(1)}, u32[]{:S(2)}, u32[]{:S(2)}) %collective-permute-start.21) | collective-permute-done | bytes 819232 | tf_op jit(solution)/shard_map/ppermute | solution.py:110
  195.2 20.3 %conditional.8 = (f32[160,2560]{1,0:T(8,128)S(1)}) conditional(s32[]{:T(128)} %bitcast.26, f32[160,2560]{1,0:T(8,128)S(1)} %fusion.14, f32[160,2560]{1,0:T(8,128)S(1)} %fusion.14, f32[160,2560]{1,0:T(8,128)S(1)} %fusion.14, f32[160,2560]{1,0:T(8,128)S(1)} %fusion.14), branch_computations={%region_3.5_spmd, %region_4.6_spmd, %region_5.7_spmd, %region_6.8_... | conditional | flops 819200 | bytes 8192048
  196.0 19.4 %collective-permute-done = bf16[160,2560]{1,0:T(8,128)(2,1)S(1)} collective-permute-done((bf16[160,2560]{1,0:T(8,128)(2,1)S(1)}, bf16[160,2560]{1,0:T(8,128)(2,1)S(1)}, u32[]{:S(2)}, u32[]{:S(2)}) %collective-permute-start) | collective-permute-done | bytes 819232 | tf_op jit(solution)/shard_map/cond/branch_0_fun/ppermute | solution.py:20
  (68 shorter events, 31.7 us)
Async XLA Ops:
  7.2 3.3 %copy-start = (f32[1,160,2560]{2,1,0:T(8,128)S(1)}, f32[1,160,2560]{2,1,0:T(8,128)}, u32[]{:S(2)}) copy-start(f32[1,160,2560]{2,1,0:T(8,128)} %param.21) | copy-start | bytes 4915204
  7.2 49.5 %all-gather.2.cloned.1.call-start = ((), (), s32[]{:S(2)}) async-start(), calls=%async_computation.1 | async-start | bytes 4096000 | tf_op jit(solution)/shard_map/all_gather | solution.py:71
  10.4 183.1 %reduce-scatter.2.cloned.1.call-start = ((), (), s32[]{:S(2)}) async-start(), calls=%async_computation.2 | async-start | bytes 4096000 | tf_op jit(solution)/shard_map/reduce_scatter | solution.py:111
  11.5 42.0 %collective-permute-start.8 = (bf16[160,2560]{1,0:T(8,128)(2,1)}, bf16[160,2560]{1,0:T(8,128)(2,1)}, u32[]{:S(2)}, u32[]{:S(2)}) collective-permute-start(bf16[160,2560]{1,0:T(8,128)(2,1)} %fusion.15), channel_id=1, source_target_pairs={{0,8},{8,0},{1,9},{9,1},{2,10},{10,2},{3,11},{11,3},{4,12},{12,4},... | collective-permute-start | bytes 2457608 | tf_op jit(solution)/shard_map/ppermute | solution.py:77
  56.7 20.0 %collective-permute-start.10 = (bf16[160,2560]{1,0:T(8,128)(2,1)}, bf16[160,2560]{1,0:T(8,128)(2,1)S(1)}, u32[]{:S(2)}, u32[]{:S(2)}) collective-permute-start(bf16[160,2560]{1,0:T(8,128)(2,1)} %collective-permute-done.8), channel_id=1, source_target_pairs={{0,6},{2,0},{4,2},{6,4},{1,7},{3,1},{5,3},{7,5},{8,14},{10,8},{12,... | collective-permute-start | bytes 2457608 | tf_op jit(solution)/shard_map/ppermute | solution.py:30
  57.7 21.4 %collective-permute-start.11 = (bf16[160,2560]{1,0:T(8,128)(2,1)}, bf16[160,2560]{1,0:T(8,128)(2,1)S(1)}, u32[]{:S(2)}, u32[]{:S(2)}) collective-permute-start(bf16[160,2560]{1,0:T(8,128)(2,1)} %collective-permute-done.8), channel_id=1, source_target_pairs={{0,2},{2,4},{4,6},{6,0},{1,3},{3,5},{5,7},{7,1},{8,10},{10,12},{12... | collective-permute-start | bytes 2457608 | tf_op jit(solution)/shard_map/ppermute | solution.py:29
  76.8 10.3 %collective-permute-start.13 = (bf16[80,2560]{1,0:T(8,128)(2,1)S(1)}, bf16[80,2560]{1,0:T(8,128)(2,1)S(1)}, u32[]{:S(2)}, u32[]{:S(2)}) collective-permute-start(bf16[80,2560]{1,0:T(8,128)(2,1)S(1)} %slice.39), channel_id=1, source_target_pairs={{0,6},{2,0},{4,2},{6,4},{1,7},{3,1},{5,3},{7,5},{8,14},{10,8},{12,... | collective-permute-start | bytes 1228808 | tf_op jit(solution)/shard_map/ppermute | solution.py:32
  79.1 11.2 %collective-permute-start.12 = (bf16[80,2560]{1,0:T(8,128)(2,1)S(1)}, bf16[80,2560]{1,0:T(8,128)(2,1)S(1)}, u32[]{:S(2)}, u32[]{:S(2)}) collective-permute-start(bf16[80,2560]{1,0:T(8,128)(2,1)S(1)} %slice.38), channel_id=1, source_target_pairs={{0,2},{2,4},{4,6},{6,0},{1,3},{3,5},{5,7},{7,1},{8,10},{10,12},{12... | collective-permute-start | bytes 1228808 | tf_op jit(solution)/shard_map/ppermute | solution.py:32
  79.1 16.0 %collective-permute-start.9 = (bf16[4,160,2560]{2,1,0:T(8,128)(2,1)}, bf16[4,160,2560]{2,1,0:T(8,128)(2,1)S(1)}, u32[]{:S(2)}, u32[]{:S(2)}) collective-permute-start(bf16[4,160,2560]{2,1,0:T(8,128)(2,1)} %all-gather.2.cloned.1.call-done), channel_id=1, source_target_pairs={{0,1},{1,0},{2,3},{3,2},{4,5},{5,4},{6,7},{7,6},{8,9},{9,8},{10,11... | collective-permute-start | bytes 9830408 | tf_op jit(solution)/shard_map/ppermute | solution.py:80
  91.8 6.1 %collective-permute-start.14 = (bf16[4,160,2560]{2,1,0:T(8,128)(2,1)S(1)}, bf16[4,160,2560]{2,1,0:T(8,128)(2,1)S(1)}, u32[]{:S(2)}, u32[]{:S(2)}) collective-permute-start(bf16[4,160,2560]{2,1,0:T(8,128)(2,1)S(1)} %pad_maximum_fusion), channel_id=1, source_target_pairs={{0,1},{1,0},{2,3},{3,2},{4,5},{5,4},{6,7},{7,6},{8,9},{9,8},{10,11... | collective-permute-start | bytes 9830408 | tf_op jit(solution)/shard_map/ppermute | solution.py:81
  96.9 2.8 %copy-start.3 = (bf16[4,160,2560]{2,1,0:T(8,128)(2,1)S(1)}, bf16[4,160,2560]{2,1,0:T(8,128)(2,1)}, u32[]{:S(2)}) copy-start(bf16[4,160,2560]{2,1,0:T(8,128)(2,1)} %all-gather.2.cloned.1.call-done) | copy-start | bytes 9830404
  96.9 2.8 %copy-start.6 = (bf16[1,384,2560]{2,1,0:T(8,128)(2,1)S(1)}, bf16[1,384,2560]{2,1,0:T(8,128)(2,1)}, u32[]{:S(2)}) copy-start(bf16[1,384,2560]{2,1,0:T(8,128)(2,1)} %param.18) | copy-start | bytes 5898244
  104.2 6.1 %copy-start.4 = (bf16[384,2560,1]{1,0,2:T(8,128)(2,1)}, bf16[384,2560,1]{1,0,2:T(8,128)(2,1)S(1)}, u32[]{:S(2)}) copy-start(bf16[384,2560,1]{1,0,2:T(8,128)(2,1)S(1)} %fusion.9) | copy-start | bytes 5898244
  106.1 6.1 %collective-permute-start.16 = (bf16[4,160,2560]{2,1,0:T(8,128)(2,1)S(1)}, bf16[4,160,2560]{2,1,0:T(8,128)(2,1)S(1)}, u32[]{:S(2)}, u32[]{:S(2)}) collective-permute-start(bf16[4,160,2560]{2,1,0:T(8,128)(2,1)S(1)} %convolution_convert_fusion), channel_id=1, source_target_pairs={{0,1},{1,0},{2,3},{3,2},{4,5},{5,4},{6,7},{7,6},{8,9},{9,8},{10,11... | collective-permute-start | bytes 9830408 | tf_op jit(solution)/shard_map/ppermute | solution.py:102
  110.0 21.9 %collective-permute-start.15 = (bf16[4,160,2560]{2,1,0:T(8,128)(2,1)}, bf16[4,160,2560]{2,1,0:T(8,128)(2,1)S(1)}, u32[]{:S(2)}, u32[]{:S(2)}) collective-permute-start(bf16[4,160,2560]{2,1,0:T(8,128)(2,1)} %convolution_convert_fusion.2), channel_id=1, source_target_pairs={{0,1},{1,0},{2,3},{3,2},{4,5},{5,4},{6,7},{7,6},{8,9},{9,8},{10,11... | collective-permute-start | bytes 9830408 | tf_op jit(solution)/shard_map/ppermute | solution.py:102
  112.8 13.1 %copy-start.1 = (f32[4,160,2560]{2,1,0:T(8,128)}, f32[4,160,2560]{2,1,0:T(8,128)S(1)}, u32[]{:S(2)}) copy-start(f32[4,160,2560]{2,1,0:T(8,128)S(1)} %get-tuple-element.49) | copy-start | bytes 19660804
  113.0 12.8 %collective-permute-start.17 = (bf16[80,2560]{1,0:T(8,128)(2,1)S(1)}, bf16[80,2560]{1,0:T(8,128)(2,1)S(1)}, u32[]{:S(2)}, u32[]{:S(2)}) collective-permute-start(bf16[80,2560]{1,0:T(8,128)(2,1)S(1)} %get-tuple-element.53), channel_id=1, source_target_pairs={{0,2},{2,4},{4,6},{6,0},{1,3},{3,5},{5,7},{7,1},{8,10},{10,12},{12... | collective-permute-start | bytes 1228808 | tf_op jit(solution)/shard_map/ppermute | solution.py:44
  113.1 12.7 %collective-permute-start.19 = (bf16[80,2560]{1,0:T(8,128)(2,1)S(1)}, bf16[80,2560]{1,0:T(8,128)(2,1)S(1)}, u32[]{:S(2)}, u32[]{:S(2)}) collective-permute-start(bf16[80,2560]{1,0:T(8,128)(2,1)S(1)} %get-tuple-element.56), channel_id=1, source_target_pairs={{0,6},{2,0},{4,2},{6,4},{1,7},{3,1},{5,3},{7,5},{8,14},{10,8},{12,... | collective-permute-start | bytes 1228808 | tf_op jit(solution)/shard_map/ppermute | solution.py:45
  125.8 4.2 %copy-start.5 = (bf16[384,2560,1]{1,0,2:T(8,128)(2,1)S(1)}, bf16[384,2560,1]{1,0,2:T(8,128)(2,1)}, u32[]{:S(2)}) copy-start(bf16[384,2560,1]{1,0,2:T(8,128)(2,1)} %copy-done.4) | copy-start | bytes 5898244
  126.1 19.7 %collective-permute-start.20 = (bf16[160,2560]{1,0:T(8,128)(2,1)S(1)}, bf16[160,2560]{1,0:T(8,128)(2,1)}, u32[]{:S(2)}, u32[]{:S(2)}) collective-permute-start(bf16[160,2560]{1,0:T(8,128)(2,1)S(1)} %pad_maximum_fusion.2), channel_id=1, source_target_pairs={{0,6},{2,0},{4,2},{6,4},{1,7},{3,1},{5,3},{7,5},{8,14},{10,8},{12,... | collective-permute-start | bytes 2457608 | tf_op jit(solution)/shard_map/ppermute | solution.py:49
  130.0 20.4 %collective-permute-start.18 = (bf16[160,2560]{1,0:T(8,128)(2,1)}, bf16[160,2560]{1,0:T(8,128)(2,1)}, u32[]{:S(2)}, u32[]{:S(2)}) collective-permute-start(bf16[160,2560]{1,0:T(8,128)(2,1)} %pad_maximum_fusion.1), channel_id=1, source_target_pairs={{0,2},{2,4},{4,6},{6,0},{1,3},{3,5},{5,7},{7,1},{8,10},{10,12},{12... | collective-permute-start | bytes 2457608 | tf_op jit(solution)/shard_map/ppermute | solution.py:48
  152.7 39.3 %collective-permute-start.21 = (bf16[160,2560]{1,0:T(8,128)(2,1)S(1)}, bf16[160,2560]{1,0:T(8,128)(2,1)S(1)}, u32[]{:S(2)}, u32[]{:S(2)}) collective-permute-start(bf16[160,2560]{1,0:T(8,128)(2,1)S(1)} %fusion.12), channel_id=1, source_target_pairs={{0,8},{8,0},{1,9},{9,1},{2,10},{10,2},{3,11},{11,3},{4,12},{12,4},... | collective-permute-start | bytes 2457608 | tf_op jit(solution)/shard_map/ppermute | solution.py:110
  159.8 3.6 %collective-permute-start.4 = (bf16[1]{0:T(256)(128)(2,1)}, bf16[1]{0:T(256)(128)(2,1)}, u32[]{:S(2)}, u32[]{:S(2)}) collective-permute-start(bf16[1]{0:T(256)(128)(2,1)} %convert_element_type.102), channel_id=1, source_target_pairs={{0,16},{16,0},{32,48},{48,32},{64,80},{80,64},{96,112},{112,96},{1... | collective-permute-start | bytes 14 | tf_op jit(solution)/shard_map/cond/branch_0_fun/ppermute | solution.py:20
  195.3 20.0 %collective-permute-start = (bf16[160,2560]{1,0:T(8,128)(2,1)S(1)}, bf16[160,2560]{1,0:T(8,128)(2,1)S(1)}, u32[]{:S(2)}, u32[]{:S(2)}) collective-permute-start(bf16[160,2560]{1,0:T(8,128)(2,1)S(1)} %convert_element_type.94), channel_id=1, source_target_pairs={{0,16},{16,0},{32,48},{48,32},{64,80},{80,64},{96,112},{112,96},{1... | collective-permute-start | bytes 2457608 | tf_op jit(solution)/shard_map/cond/branch_0_fun/ppermute | solution.py:20
  (4 other events, 8.0 us)
Sparse Core Ops, SparseCore 0:
  10.6 46.0 all-gather.1
  152.8 40.7 reduce-scatter.1
